TPU v7x, 32 devices: a whole 2x2x4 slice. The times are simulated.
32 devices in a mesh: dom: 4 (over y, x), orb: 8 (over z, core).
Axes of the slice: x: 2, y: 2, z: 4, core: 2. Of those that a mesh axis runs over, the one named last changes fastest.
Arguments:
- orbitals: float32 [16, 24, 32, 256], P('orb', 'dom'), may hold values from -12 to 12
- potential: float32 [24, 32, 256], P('dom'), may hold values from 0 to 3
- degrees: int32 [8], P('orb'), may hold values from 1 to 3
Outputs:
- filtered: bfloat16 [16, 24, 32, 256], P('orb', 'dom')
- correlation: float32 [16, 16], P('orb')
All inputs are finite; a program needn't handle non-finite values.
Results may differ from a plain program's by a relative error of at most 0.0004.
Values may be sent and summed in bfloat16 or wider, within the bound.
No kernel may reach another device: no remote copies, remote signals or barrier semaphores. Data moves between devices by JAX's collectives and lax.ppermute only.
A program may use at most 64 MiB of HBM per device.

v0:
```python
import jax
import jax.numpy as jnp
from jax import lax
from jax.sharding import PartitionSpec as P

DEG_MAX = 3


CENTER_COEF = -5369.0 / 1800.0
STENCIL = (12.0 / 7.0, -15.0 / 56.0, 10.0 / 189.0, -1.0 / 112.0, 2.0 / 1925.0, -1.0 / 16632.0)
SHIFT_C = 8.5
HALF_W = 4.5


def with_halo(cells, sides, width):
    for axis, dim in sides:
        count = lax.axis_size(axis)
        ends = count - 1
        head = lax.slice_in_dim(cells, 0, width, axis=dim)
        tail = lax.slice_in_dim(cells, cells.shape[dim] - width, cells.shape[dim], axis=dim)
        cells = jnp.concatenate(
            [
                lax.ppermute(tail, axis, [(i, (i + 1) % count) for i in range(ends)]),
                cells,
                lax.ppermute(head, axis, [((i + 1) % count, i) for i in range(ends)]),
            ],
            axis=dim,
        )
    return cells


def hamiltonian(field, potential):
    padded = with_halo(field, (("dom", 1),), 6)
    planes = field.shape[1]
    laplace = 3.0 * CENTER_COEF * field
    for offset, weight in enumerate(STENCIL, 1):
        beside_all = (
            padded[:, 6 + offset : 6 + offset + planes]
            + padded[:, 6 - offset : 6 - offset + planes]
        )
        beside_all = beside_all + jnp.roll(field, offset, 2) + jnp.roll(field, -offset, 2)
        beside_all = beside_all + jnp.roll(field, offset, 3) + jnp.roll(field, -offset, 3)
        laplace = laplace + weight * beside_all
    return -0.5 * laplace + potential * field


def inner_rows(left, right):
    return lax.dot_general(
        left, right, (((1,), (1,)), ((), ())), preferred_element_type=jnp.float32
    )


def per_device(orbitals, potential, degrees):
    block_orbs = orbitals.shape[0]
    degree = degrees.reshape(1, 1, 1, 1)
    first = (hamiltonian(orbitals, potential) - SHIFT_C * orbitals) / HALF_W
    previous, current, picked = (orbitals, first, first)
    for order in range(2, DEG_MAX + 1):
        following = 2.0 * (hamiltonian(current, potential) - SHIFT_C * current) / HALF_W - previous
        picked = jnp.where(degree >= order, following, picked)
        previous, current = (current, following)
    filtered = picked.astype(jnp.bfloat16)
    cell_count = orbitals.shape[1] * orbitals.shape[2] * orbitals.shape[3]
    total_cells = float(cell_count * lax.axis_size("dom"))
    flattened = filtered.reshape(block_orbs, cell_count)
    mixed = lax.all_to_all(flattened, "orb", split_axis=1, concat_axis=0, tiled=True)
    partial_gram = inner_rows(mixed, mixed)
    row_block = lax.psum_scatter(partial_gram, "orb", scatter_dimension=0, tiled=True)
    correlation = lax.psum(row_block, "dom") / total_cells
    return (filtered, correlation)


def solution(mesh):
    placed = (P("orb", "dom", None, None), P("dom", None, None), P("orb"))
    return jax.shard_map(
        per_device,
        mesh=mesh,
        in_specs=placed,
        out_specs=(P("orb", "dom", None, None), P("orb", None)),
        check_vma=False,
    )
```

profile of v0, /device:TPU:0, one launch (start us, length us, event | category | flops | bytes accessed | tf_op | source)
XLA Modules:
  0.0 114.1 jit_solution(8168870975486236169)
XLA Ops:
  0.6 5.0 %collective-permute-start.1 = (f32[2,6,32,256]{3,2,1,0:T(8,128)}, f32[2,6,32,256]{3,2,1,0:T(8,128)S(1)}, u32[]{:S(2)}, u32[]{:S(2)}) collective-permute-start(f32[2,6,32,256]{3,2,1,0:T(8,128)} %param.3), channel_id=1, source_target_pairs={{0,8},{8,16},{16,24},{1,9},{9,17},{17,25},{2,10},{10,18},{18,26},{... | collective-permute-start | bytes 1179656 | tf_op jit(solution)/shard_map/ppermute | solution.py:23
  5.7 1.3 %collective-permute-start = (f32[2,6,32,256]{3,2,1,0:T(8,128)}, f32[2,6,32,256]{3,2,1,0:T(8,128)S(1)}, u32[]{:S(2)}, u32[]{:S(2)}) collective-permute-start(f32[2,6,32,256]{3,2,1,0:T(8,128)} %param.3), channel_id=1, source_target_pairs={{8,0},{16,8},{24,16},{9,1},{17,9},{25,17},{10,2},{18,10},{26,18},{... | collective-permute-start | bytes 1179656 | tf_op jit(solution)/shard_map/ppermute | solution.py:25
  7.0 1.2 %fusion.196 = (f32[2,6,31,256]{3,2,1,0:T(8,128)S(1)}, f32[2,6,31,256]{3,2,1,0:T(8,128)S(1)}) fusion(f32[2,6,32,256]{3,2,1,0:T(8,128)} %param.3), kind=kLoop, calls=%fused_computation.247 | loop fusion | bytes 1523712 | tf_op jit(solution)/shard_map/jit(_roll_static)/slice | solution.py:41
  8.4 0.2 fusion.202
  8.7 0.2 fusion.206
  8.9 0.2 fusion.210
  9.2 0.2 fusion.214
  9.4 0.2 fusion.218
  10.4 0.9 copy-done.1
  12.0 2.3 %collective-permute-done.1 = f32[2,6,32,256]{3,2,1,0:T(8,128)S(1)} collective-permute-done((f32[2,6,32,256]{3,2,1,0:T(8,128)}, f32[2,6,32,256]{3,2,1,0:T(8,128)S(1)}, u32[]{:S(2)}, u32[]{:S(2)}) %collective-permute-start.1) | collective-permute-done | bytes 393248 | tf_op jit(solution)/shard_map/ppermute | solution.py:23
  14.4 10.1 %collective-permute-done = f32[2,6,32,256]{3,2,1,0:T(8,128)S(1)} collective-permute-done((f32[2,6,32,256]{3,2,1,0:T(8,128)}, f32[2,6,32,256]{3,2,1,0:T(8,128)S(1)}, u32[]{:S(2)}, u32[]{:S(2)}) %collective-permute-start) | collective-permute-done | bytes 393248 | tf_op jit(solution)/shard_map/ppermute | solution.py:25
  24.6 2.5 %broadcast_multiply_fusion = (f32[2,6,32,256]{3,2,1,0:T(8,128)S(1)}, f32[2,6,32,256]{3,2,1,0:T(8,128)S(1)}) fusion(f32[2,6,32,256]{3,2,1,0:T(8,128)S(1)} %copy-done, f32[6,32,256]{2,1,0:T(8,128)S(1)} %copy-done.1, f32[2,6,32,6]{3,2,1,0:T(8,128)S(1)} %get-tuple-element.147, f32[2,6,32,250]{3,2,1,0:T(8,128)S(1)} %get-tuple-element.149, ...), kind=kLoop, calls=%fused_computation.190 | loop fusion | flops 7176192 | bytes 15532032 | tf_op jit(solution)/shard_map/div | solution.py:56
  27.3 0.2 fusion.175
  27.8 0.2 fusion.183
  28.1 0.2 fusion.187
  29.4 1.3 %collective-permute-start.2 = (f32[2,6,32,256]{3,2,1,0:T(8,128)S(1)}, f32[2,6,32,256]{3,2,1,0:T(8,128)S(1)}, u32[]{:S(2)}, u32[]{:S(2)}) collective-permute-start(f32[2,6,32,256]{3,2,1,0:T(8,128)S(1)} %get-tuple-element.2), channel_id=1, source_target_pairs={{8,0},{16,8},{24,16},{9,1},{17,9},{25,17},{10,2},{18,10},{26,18},{... | collective-permute-start | bytes 1179656 | tf_op jit(solution)/shard_map/ppermute | solution.py:25
  30.7 4.6 %collective-permute-start.3 = (f32[2,6,32,256]{3,2,1,0:T(8,128)S(1)}, f32[2,6,32,256]{3,2,1,0:T(8,128)S(1)}, u32[]{:S(2)}, u32[]{:S(2)}) collective-permute-start(f32[2,6,32,256]{3,2,1,0:T(8,128)S(1)} %get-tuple-element.2), channel_id=1, source_target_pairs={{0,8},{8,16},{16,24},{1,9},{9,17},{17,25},{2,10},{10,18},{18,26},{... | collective-permute-start | bytes 1179656 | tf_op jit(solution)/shard_map/ppermute | solution.py:23
  35.3 7.9 %collective-permute-done.2 = f32[2,6,32,256]{3,2,1,0:T(8,128)S(1)} collective-permute-done((f32[2,6,32,256]{3,2,1,0:T(8,128)S(1)}, f32[2,6,32,256]{3,2,1,0:T(8,128)S(1)}, u32[]{:S(2)}, u32[]{:S(2)}) %collective-permute-start.2) | collective-permute-done | bytes 393248 | tf_op jit(solution)/shard_map/ppermute | solution.py:25
  43.2 2.4 %fusion.58 = f32[2,6,32,256]{3,2,1,0:T(8,128)S(1)} fusion(f32[2,6,32,256]{3,2,1,0:T(8,128)S(1)} %copy-done, f32[2,6,32,256]{3,2,1,0:T(8,128)S(1)} %collective-permute-done.3, f32[2,6,32,256]{3,2,1,0:T(8,128)S(1)} %get-tuple-element.2, f32[2,6,32,256]{3,2,1,0:T(8,128)S(1)} %collective-permute-done.2, f32[2,6,31,256]{3,2,1,0:T(8,128)S(1)} %get-tuple-element.97, ...), kind=kLoop, calls=%fused_computation.90 | loop fusion | flops 8257536 | bytes 11993088 | tf_op jit(solution)/shard_map/sub | solution.py:59
  47.1 1.3 %collective-permute-start.4 = (f32[2,6,32,256]{3,2,1,0:T(8,128)S(1)}, f32[2,6,32,256]{3,2,1,0:T(8,128)S(1)}, u32[]{:S(2)}, u32[]{:S(2)}) collective-permute-start(f32[2,6,32,256]{3,2,1,0:T(8,128)S(1)} %fusion.58), channel_id=1, source_target_pairs={{8,0},{16,8},{24,16},{9,1},{17,9},{25,17},{10,2},{18,10},{26,18},{... | collective-permute-start | bytes 1179656 | tf_op jit(solution)/shard_map/ppermute | solution.py:25
  48.4 8.5 %collective-permute-start.5 = (f32[2,6,32,256]{3,2,1,0:T(8,128)S(1)}, f32[2,6,32,256]{3,2,1,0:T(8,128)S(1)}, u32[]{:S(2)}, u32[]{:S(2)}) collective-permute-start(f32[2,6,32,256]{3,2,1,0:T(8,128)S(1)} %fusion.58), channel_id=1, source_target_pairs={{0,8},{8,16},{16,24},{1,9},{9,17},{17,25},{2,10},{10,18},{18,26},{... | collective-permute-start | bytes 1179656 | tf_op jit(solution)/shard_map/ppermute | solution.py:23
  57.9 7.1 %collective-permute-done.4 = f32[2,6,32,256]{3,2,1,0:T(8,128)S(1)} collective-permute-done((f32[2,6,32,256]{3,2,1,0:T(8,128)S(1)}, f32[2,6,32,256]{3,2,1,0:T(8,128)S(1)}, u32[]{:S(2)}, u32[]{:S(2)}) %collective-permute-start.4) | collective-permute-done | bytes 393248 | tf_op jit(solution)/shard_map/ppermute | solution.py:25
  65.0 2.5 %fusion.145 = bf16[2,6,32,256]{3,2,1,0:T(8,128)(2,1)S(1)} fusion(f32[2,6,32,256]{3,2,1,0:T(8,128)S(1)} %fusion.58, f32[2,6,32,6]{3,2,1,0:T(8,128)S(1)} %get-tuple-element.49, f32[2,6,32,250]{3,2,1,0:T(8,128)S(1)} %get-tuple-element.51, f32[2,6,32,250]{3,2,1,0:T(8,128)S(1)} %get-tuple-element.50, f32[2,6,32,6]{3,2,1,0:T(8,128)S(1)} %get-tuple-element.48, ...), kind=kLoop, calls=%fused_computation.189 | loop fusion | flops 8650752 | bytes 11403266 | tf_op jit(solution)/shard_map/convert_element_type | solution.py:62
  67.6 0.9 copy.6
  68.5 4.9 %all-to-all-start = ((bf16[2,8,6144]{2,0,1:T(2,128)(2,1)}), bf16[2,8,6144]{2,0,1:T(2,128)(2,1)S(1)}, u32[]{:S(2)}, u32[]{:S(2)}) async-start(bf16[2,8,6144]{2,0,1:T(2,128)(2,1)} %copy.6), calls=%async_computation | async-start | bytes 393216 | tf_op jit(solution)/shard_map/all_to_all | solution.py:66
  73.4 0.7 copy-done.3
  74.0 0.6 dynamic-slice
  75.3 6.4 %all-to-all-done = bf16[2,8,6144]{2,0,1:T(2,128)(2,1)S(1)} async-done(((bf16[2,8,6144]{2,0,1:T(2,128)(2,1)}), bf16[2,8,6144]{2,0,1:T(2,128)(2,1)S(1)}, u32[]{:S(2)}, u32[]{:S(2)}) %all-to-all-start) | async-done | bytes 196640 | tf_op jit(solution)/shard_map/all_to_all | solution.py:66
  81.8 0.2 fusion.219
  82.0 14.8 %all-reduce = f32[16,16]{1,0:T(8,128)S(1)} all-reduce(f32[16,16]{1,0:T(8,128)S(1)} %fusion.219), channel_id=2, replica_groups=mesh['dom'=4,'orb'=8] {'orb'}, use_global_device_ids=true, to_apply=%region_0.1.clone | all-reduce | flops 256 | bytes 2048
  96.8 16.7 %psum.7 = f32[2,16]{1,0:T(2,128)S(1)} all-reduce(f32[2,16]{1,0:T(2,128)S(1)} %constant_dynamic-slice_fusion), channel_id=1, replica_groups=mesh['dom'=4,'orb'=8] {'dom'}, use_global_device_ids=true, to_apply=%region_1.2 | all-reduce | flops 32 | bytes 256 | tf_op jit(solution)/shard_map/psum | solution.py:69
  113.5 0.6 broadcast_multiply_fusion.2
  (78 shorter events, 5.7 us)
Async XLA Ops:
  0.6 7.5 %copy-start = (f32[2,6,32,256]{3,2,1,0:T(8,128)S(1)}, f32[2,6,32,256]{3,2,1,0:T(8,128)}, u32[]{:S(2)}) copy-start(f32[2,6,32,256]{3,2,1,0:T(8,128)} %param.3) | copy-start | bytes 1179652
  0.6 13.7 %collective-permute-start.1 = (f32[2,6,32,256]{3,2,1,0:T(8,128)}, f32[2,6,32,256]{3,2,1,0:T(8,128)S(1)}, u32[]{:S(2)}, u32[]{:S(2)}) collective-permute-start(f32[2,6,32,256]{3,2,1,0:T(8,128)} %param.3), channel_id=1, source_target_pairs={{0,8},{8,16},{16,24},{1,9},{9,17},{17,25},{2,10},{10,18},{18,26},{... | collective-permute-start | bytes 1179656 | tf_op jit(solution)/shard_map/ppermute | solution.py:23
  5.7 18.9 %collective-permute-start = (f32[2,6,32,256]{3,2,1,0:T(8,128)}, f32[2,6,32,256]{3,2,1,0:T(8,128)S(1)}, u32[]{:S(2)}, u32[]{:S(2)}) collective-permute-start(f32[2,6,32,256]{3,2,1,0:T(8,128)} %param.3), channel_id=1, source_target_pairs={{8,0},{16,8},{24,16},{9,1},{17,9},{25,17},{10,2},{18,10},{26,18},{... | collective-permute-start | bytes 1179656 | tf_op jit(solution)/shard_map/ppermute | solution.py:25
  10.4 0.9 copy-start.1
  29.4 13.9 %collective-permute-start.2 = (f32[2,6,32,256]{3,2,1,0:T(8,128)S(1)}, f32[2,6,32,256]{3,2,1,0:T(8,128)S(1)}, u32[]{:S(2)}, u32[]{:S(2)}) collective-permute-start(f32[2,6,32,256]{3,2,1,0:T(8,128)S(1)} %get-tuple-element.2), channel_id=1, source_target_pairs={{8,0},{16,8},{24,16},{9,1},{17,9},{25,17},{10,2},{18,10},{26,18},{... | collective-permute-start | bytes 1179656 | tf_op jit(solution)/shard_map/ppermute | solution.py:25
  30.7 12.6 %collective-permute-start.3 = (f32[2,6,32,256]{3,2,1,0:T(8,128)S(1)}, f32[2,6,32,256]{3,2,1,0:T(8,128)S(1)}, u32[]{:S(2)}, u32[]{:S(2)}) collective-permute-start(f32[2,6,32,256]{3,2,1,0:T(8,128)S(1)} %get-tuple-element.2), channel_id=1, source_target_pairs={{0,8},{8,16},{16,24},{1,9},{9,17},{17,25},{2,10},{10,18},{18,26},{... | collective-permute-start | bytes 1179656 | tf_op jit(solution)/shard_map/ppermute | solution.py:23
  47.1 17.8 %collective-permute-start.4 = (f32[2,6,32,256]{3,2,1,0:T(8,128)S(1)}, f32[2,6,32,256]{3,2,1,0:T(8,128)S(1)}, u32[]{:S(2)}, u32[]{:S(2)}) collective-permute-start(f32[2,6,32,256]{3,2,1,0:T(8,128)S(1)} %fusion.58), channel_id=1, source_target_pairs={{8,0},{16,8},{24,16},{9,1},{17,9},{25,17},{10,2},{18,10},{26,18},{... | collective-permute-start | bytes 1179656 | tf_op jit(solution)/shard_map/ppermute | solution.py:25
  48.4 16.6 %collective-permute-start.5 = (f32[2,6,32,256]{3,2,1,0:T(8,128)S(1)}, f32[2,6,32,256]{3,2,1,0:T(8,128)S(1)}, u32[]{:S(2)}, u32[]{:S(2)}) collective-permute-start(f32[2,6,32,256]{3,2,1,0:T(8,128)S(1)} %fusion.58), channel_id=1, source_target_pairs={{0,8},{8,16},{16,24},{1,9},{9,17},{17,25},{2,10},{10,18},{18,26},{... | collective-permute-start | bytes 1179656 | tf_op jit(solution)/shard_map/ppermute | solution.py:23
  67.5 1.0 copy-start.2
  68.5 13.2 %all-to-all-start = ((bf16[2,8,6144]{2,0,1:T(2,128)(2,1)}), bf16[2,8,6144]{2,0,1:T(2,128)(2,1)S(1)}, u32[]{:S(2)}, u32[]{:S(2)}) async-start(bf16[2,8,6144]{2,0,1:T(2,128)(2,1)} %copy.6), calls=%async_computation | async-start | bytes 393216 | tf_op jit(solution)/shard_map/all_to_all | solution.py:66
  73.4 0.7 copy-start.3
where the time goes:
time: 115 us; the launch traced here: 114 us
  waiting for transfers between devices  33.8 us (29%)
  blocking collectives  31.5 us (27%)
  starting transfers between devices  26.9 us (23%)
  local copies, waits for them, and re-layouts  11.3 us (10%)
  other arithmetic  8 us (7%)
  between operations  2.42 us (2%)
    ppermute x3, waiting for transfers between devices, with_halo(): lax.ppermute(head, axis, [((i + 1) % count, i) for i in range(ends)])  25.1 us
    ppermute x3, starting transfers between devices, with_halo(): lax.ppermute(tail, axis, [(i, (i + 1) % count) for i in range(ends)])  18.1 us
    psum x1, blocking collectives, per_device(): correlation = lax.psum(row_block, 'dom') / total_cells  16.7 us
    unnamed x1, blocking collectives  14.8 us
    all_to_all x1, waiting for transfers between devices, per_device(): lax.all_to_all(flattened, 'orb', split_axis=1, concat_axis=0, tiled=True)  6.42 us
    all_to_all x1, starting transfers between devices, per_device(): lax.all_to_all(flattened, 'orb', split_axis=1, concat_axis=0, tiled=True)  4.88 us
    ppermute x3, starting transfers between devices, with_halo(): lax.ppermute(head, axis, [((i + 1) % count, i) for i in range(ends)])  3.88 us
    slice x24, local copies, waits for them, and re-layouts, hamiltonian(): jnp.roll(field, offset, 3)  3.52 us
  transfers between devices with their start and end apart: 7, of which 5 were waited for; matrix products, arithmetic and copies ran while one was open for 4% of the time, Pallas kernels for 0%

commit v1 on v0

--- a/solution.py
+++ b/solution.py
@@ -61,12 +61,15 @@
         previous, current = (current, following)
     filtered = picked.astype(jnp.bfloat16)
     cell_count = orbitals.shape[1] * orbitals.shape[2] * orbitals.shape[3]
-    total_cells = float(cell_count * lax.axis_size("dom"))
+    n_orb, n_dom = lax.axis_size("orb"), lax.axis_size("dom")
+    total_cells = float(cell_count * n_dom)
     flattened = filtered.reshape(block_orbs, cell_count)
     mixed = lax.all_to_all(flattened, "orb", split_axis=1, concat_axis=0, tiled=True)
     partial_gram = inner_rows(mixed, mixed)
-    row_block = lax.psum_scatter(partial_gram, "orb", scatter_dimension=0, tiled=True)
-    correlation = lax.psum(row_block, "dom") / total_cells
+    rows = partial_gram.reshape(n_orb, 1, block_orbs, -1)
+    sends = jnp.broadcast_to(rows, (n_orb, n_dom) + rows.shape[2:]).reshape((n_orb * n_dom,) + rows.shape[2:])
+    gathered = lax.all_to_all(sends, ("orb", "dom"), split_axis=0, concat_axis=0, tiled=True)
+    correlation = gathered.sum(axis=0) / total_cells
     return (filtered, correlation)
 
 

time: 115 us -> 100 us (0.87)
  waiting for transfers between devices: 33.8 us -> 27.4 us
  starting transfers between devices: 26.9 us -> 22 us
  local copies, waits for them, and re-layouts: 11.3 us -> 9.99 us
    all_to_all x0 -> x2, blocking collectives: none -> 30.4 us  [the longest x1 17.4 us: per_device(): lax.all_to_all(sends, ('orb', 'dom'), split_axis=0, concat_axis=0, tiled=...]
    psum x1 -> x0, blocking collectives: 16.7 us -> none  [per_device(): correlation = lax.psum(row_block, 'dom') / total_cells]
    unnamed x1 -> x0, blocking collectives: 14.8 us -> none
    all_to_all x1 -> x0, waiting for transfers between devices: 6.42 us -> none  [per_device(): lax.all_to_all(flattened, 'orb', split_axis=1, concat_axis=0, tiled=True)]
    all_to_all x1 -> x0, starting transfers between devices: 4.88 us -> none  [per_device(): lax.all_to_all(flattened, 'orb', split_axis=1, concat_axis=0, tiled=True)]
  transfers between devices with their start and end apart: 7 -> 6, of which waited for: 5 -> 4; matrix products, arithmetic and copies ran while one was open for 4% -> 5% of each run, Pallas kernels for 0% -> 0%
where the time goes in v1:
time: 100 us; the launch traced here: 99.8 us
  blocking collectives  30.4 us (30%)
  waiting for transfers between devices  27.4 us (27%)
  starting transfers between devices  22 us (22%)
  local copies, waits for them, and re-layouts  9.99 us (10%)
  other arithmetic  8.04 us (8%)
  between operations  1.78 us (2%)
    ppermute x3, waiting for transfers between devices, with_halo(): lax.ppermute(head, axis, [((i + 1) % count, i) for i in range(ends)])  25.1 us
    ppermute x3, starting transfers between devices, with_halo(): lax.ppermute(tail, axis, [(i, (i + 1) % count) for i in range(ends)])  18.1 us
    all_to_all x1, blocking collectives, per_device(): lax.all_to_all(sends, ('orb', 'dom'), split_axis=0, concat_axis=0, tiled=...  17.4 us
    all_to_all x1, blocking collectives, per_device(): lax.all_to_all(flattened, 'orb', split_axis=1, concat_axis=0, tiled=True)  13 us
    ppermute x3, starting transfers between devices, with_halo(): lax.ppermute(head, axis, [((i + 1) % count, i) for i in range(ends)])  3.88 us
    slice x24, local copies, waits for them, and re-layouts, hamiltonian(): jnp.roll(field, offset, 3)  3.52 us
    convert_element_type x1, other arithmetic, per_device(): filtered = picked.astype(jnp.bfloat16)  2.52 us
    div x1, other arithmetic, per_device(): first = (hamiltonian(orbitals, potential) - SHIFT_C * orbitals) / HALF_W  2.45 us
  transfers between devices with their start and end apart: 6, of which 4 were waited for; matrix products, arithmetic and copies ran while one was open for 5% of the time, Pallas kernels for 0%

profile of v1, /device:TPU:0, one launch (start us, length us, event | category | flops | bytes accessed | tf_op | source)
XLA Modules:
  0.0 99.8 jit_solution(12293451328161675504)
XLA Ops:
  0.6 5.0 %collective-permute-start.1 = (f32[2,6,32,256]{3,2,1,0:T(8,128)}, f32[2,6,32,256]{3,2,1,0:T(8,128)S(1)}, u32[]{:S(2)}, u32[]{:S(2)}) collective-permute-start(f32[2,6,32,256]{3,2,1,0:T(8,128)} %param.3), channel_id=1, source_target_pairs={{0,8},{8,16},{16,24},{1,9},{9,17},{17,25},{2,10},{10,18},{18,26},{... | collective-permute-start | bytes 1179656 | tf_op jit(solution)/shard_map/ppermute | solution.py:23
  5.7 1.3 %collective-permute-start = (f32[2,6,32,256]{3,2,1,0:T(8,128)}, f32[2,6,32,256]{3,2,1,0:T(8,128)S(1)}, u32[]{:S(2)}, u32[]{:S(2)}) collective-permute-start(f32[2,6,32,256]{3,2,1,0:T(8,128)} %param.3), channel_id=1, source_target_pairs={{8,0},{16,8},{24,16},{9,1},{17,9},{25,17},{10,2},{18,10},{26,18},{... | collective-permute-start | bytes 1179656 | tf_op jit(solution)/shard_map/ppermute | solution.py:25
  7.0 1.2 %fusion.197 = (f32[2,6,31,256]{3,2,1,0:T(8,128)S(1)}, f32[2,6,31,256]{3,2,1,0:T(8,128)S(1)}) fusion(f32[2,6,32,256]{3,2,1,0:T(8,128)} %param.3), kind=kLoop, calls=%fused_computation.248 | loop fusion | bytes 1523712 | tf_op jit(solution)/shard_map/jit(_roll_static)/slice | solution.py:41
  8.4 0.2 fusion.203
  8.7 0.2 fusion.207
  8.9 0.2 fusion.211
  9.2 0.2 fusion.215
  9.4 0.2 fusion.219
  10.4 0.9 copy-done.1
  12.0 2.3 %collective-permute-done.1 = f32[2,6,32,256]{3,2,1,0:T(8,128)S(1)} collective-permute-done((f32[2,6,32,256]{3,2,1,0:T(8,128)}, f32[2,6,32,256]{3,2,1,0:T(8,128)S(1)}, u32[]{:S(2)}, u32[]{:S(2)}) %collective-permute-start.1) | collective-permute-done | bytes 393248 | tf_op jit(solution)/shard_map/ppermute | solution.py:23
  14.4 10.1 %collective-permute-done = f32[2,6,32,256]{3,2,1,0:T(8,128)S(1)} collective-permute-done((f32[2,6,32,256]{3,2,1,0:T(8,128)}, f32[2,6,32,256]{3,2,1,0:T(8,128)S(1)}, u32[]{:S(2)}, u32[]{:S(2)}) %collective-permute-start) | collective-permute-done | bytes 393248 | tf_op jit(solution)/shard_map/ppermute | solution.py:25
  24.6 2.5 %broadcast_multiply_fusion = (f32[2,6,32,256]{3,2,1,0:T(8,128)S(1)}, f32[2,6,32,256]{3,2,1,0:T(8,128)S(1)}) fusion(f32[2,6,32,256]{3,2,1,0:T(8,128)S(1)} %copy-done, f32[6,32,256]{2,1,0:T(8,128)S(1)} %copy-done.1, f32[2,6,32,6]{3,2,1,0:T(8,128)S(1)} %get-tuple-element.147, f32[2,6,32,250]{3,2,1,0:T(8,128)S(1)} %get-tuple-element.149, ...), kind=kLoop, calls=%fused_computation.191 | loop fusion | flops 7176192 | bytes 15532032 | tf_op jit(solution)/shard_map/div | solution.py:56
  27.3 0.2 fusion.176
  27.8 0.2 fusion.184
  28.1 0.2 fusion.188
  29.4 1.3 %collective-permute-start.2 = (f32[2,6,32,256]{3,2,1,0:T(8,128)S(1)}, f32[2,6,32,256]{3,2,1,0:T(8,128)S(1)}, u32[]{:S(2)}, u32[]{:S(2)}) collective-permute-start(f32[2,6,32,256]{3,2,1,0:T(8,128)S(1)} %get-tuple-element.2), channel_id=1, source_target_pairs={{8,0},{16,8},{24,16},{9,1},{17,9},{25,17},{10,2},{18,10},{26,18},{... | collective-permute-start | bytes 1179656 | tf_op jit(solution)/shard_map/ppermute | solution.py:25
  30.7 4.6 %collective-permute-start.3 = (f32[2,6,32,256]{3,2,1,0:T(8,128)S(1)}, f32[2,6,32,256]{3,2,1,0:T(8,128)S(1)}, u32[]{:S(2)}, u32[]{:S(2)}) collective-permute-start(f32[2,6,32,256]{3,2,1,0:T(8,128)S(1)} %get-tuple-element.2), channel_id=1, source_target_pairs={{0,8},{8,16},{16,24},{1,9},{9,17},{17,25},{2,10},{10,18},{18,26},{... | collective-permute-start | bytes 1179656 | tf_op jit(solution)/shard_map/ppermute | solution.py:23
  35.3 7.9 %collective-permute-done.2 = f32[2,6,32,256]{3,2,1,0:T(8,128)S(1)} collective-permute-done((f32[2,6,32,256]{3,2,1,0:T(8,128)S(1)}, f32[2,6,32,256]{3,2,1,0:T(8,128)S(1)}, u32[]{:S(2)}, u32[]{:S(2)}) %collective-permute-start.2) | collective-permute-done | bytes 393248 | tf_op jit(solution)/shard_map/ppermute | solution.py:25
  43.2 2.4 %fusion.58 = f32[2,6,32,256]{3,2,1,0:T(8,128)S(1)} fusion(f32[2,6,32,256]{3,2,1,0:T(8,128)S(1)} %copy-done, f32[2,6,32,256]{3,2,1,0:T(8,128)S(1)} %collective-permute-done.3, f32[2,6,32,256]{3,2,1,0:T(8,128)S(1)} %get-tuple-element.2, f32[2,6,32,256]{3,2,1,0:T(8,128)S(1)} %collective-permute-done.2, f32[2,6,31,256]{3,2,1,0:T(8,128)S(1)} %get-tuple-element.97, ...), kind=kLoop, calls=%fused_computation.90 | loop fusion | flops 8257536 | bytes 11993088 | tf_op jit(solution)/shard_map/sub | solution.py:59
  45.9 0.2 fusion.155
  46.2 0.2 fusion.159
  47.1 1.3 %collective-permute-start.4 = (f32[2,6,32,256]{3,2,1,0:T(8,128)S(1)}, f32[2,6,32,256]{3,2,1,0:T(8,128)S(1)}, u32[]{:S(2)}, u32[]{:S(2)}) collective-permute-start(f32[2,6,32,256]{3,2,1,0:T(8,128)S(1)} %fusion.58), channel_id=1, source_target_pairs={{8,0},{16,8},{24,16},{9,1},{17,9},{25,17},{10,2},{18,10},{26,18},{... | collective-permute-start | bytes 1179656 | tf_op jit(solution)/shard_map/ppermute | solution.py:25
  48.4 8.5 %collective-permute-start.5 = (f32[2,6,32,256]{3,2,1,0:T(8,128)S(1)}, f32[2,6,32,256]{3,2,1,0:T(8,128)S(1)}, u32[]{:S(2)}, u32[]{:S(2)}) collective-permute-start(f32[2,6,32,256]{3,2,1,0:T(8,128)S(1)} %fusion.58), channel_id=1, source_target_pairs={{0,8},{8,16},{16,24},{1,9},{9,17},{17,25},{2,10},{10,18},{18,26},{... | collective-permute-start | bytes 1179656 | tf_op jit(solution)/shard_map/ppermute | solution.py:23
  57.9 7.1 %collective-permute-done.4 = f32[2,6,32,256]{3,2,1,0:T(8,128)S(1)} collective-permute-done((f32[2,6,32,256]{3,2,1,0:T(8,128)S(1)}, f32[2,6,32,256]{3,2,1,0:T(8,128)S(1)}, u32[]{:S(2)}, u32[]{:S(2)}) %collective-permute-start.4) | collective-permute-done | bytes 393248 | tf_op jit(solution)/shard_map/ppermute | solution.py:25
  65.0 2.5 %fusion.145 = bf16[2,6,32,256]{3,2,1,0:T(8,128)(2,1)S(1)} fusion(f32[2,6,32,256]{3,2,1,0:T(8,128)S(1)} %fusion.58, f32[2,6,32,6]{3,2,1,0:T(8,128)S(1)} %get-tuple-element.49, f32[2,6,32,250]{3,2,1,0:T(8,128)S(1)} %get-tuple-element.51, f32[2,6,32,250]{3,2,1,0:T(8,128)S(1)} %get-tuple-element.50, f32[2,6,32,6]{3,2,1,0:T(8,128)S(1)} %get-tuple-element.48, ...), kind=kLoop, calls=%fused_computation.189 | loop fusion | flops 8650752 | bytes 11403266 | tf_op jit(solution)/shard_map/convert_element_type | solution.py:62
  67.6 0.2 copy.22
  67.8 0.4 copy-done.2
  68.2 13.0 %all_to_all.24 = bf16[2,8,6144]{2,0,1:T(2,128)(2,1)S(1)} all-to-all(bf16[2,8,6144]{2,0,1:T(2,128)(2,1)S(1)} %copy.22), channel_id=1, replica_groups=mesh['dom'=4,'orb'=8] {'orb'}, dimensions={1} | all-to-all | bytes 393216 | tf_op jit(solution)/shard_map/all_to_all | solution.py:67
  81.2 0.2 copy.24
  81.5 0.2 fusion.146
  81.8 17.4 %all_to_all.25 = f32[32,2,16]{2,1,0:T(2,128)S(1)} all-to-all(f32[32,2,16]{2,1,0:T(2,128)S(1)} %copy.25), channel_id=1, replica_groups=mesh['dom'=4,'orb'=8] {'orb','dom'}, dimensions={0} | all-to-all | bytes 8192 | tf_op jit(solution)/shard_map/all_to_all | solution.py:71
  99.3 0.6 broadcast_multiply_fusion.2
  (77 shorter events, 5.5 us)
Async XLA Ops:
  0.6 7.5 %copy-start = (f32[2,6,32,256]{3,2,1,0:T(8,128)S(1)}, f32[2,6,32,256]{3,2,1,0:T(8,128)}, u32[]{:S(2)}) copy-start(f32[2,6,32,256]{3,2,1,0:T(8,128)} %param.3) | copy-start | bytes 1179652
  0.6 13.7 %collective-permute-start.1 = (f32[2,6,32,256]{3,2,1,0:T(8,128)}, f32[2,6,32,256]{3,2,1,0:T(8,128)S(1)}, u32[]{:S(2)}, u32[]{:S(2)}) collective-permute-start(f32[2,6,32,256]{3,2,1,0:T(8,128)} %param.3), channel_id=1, source_target_pairs={{0,8},{8,16},{16,24},{1,9},{9,17},{17,25},{2,10},{10,18},{18,26},{... | collective-permute-start | bytes 1179656 | tf_op jit(solution)/shard_map/ppermute | solution.py:23
  5.7 18.9 %collective-permute-start = (f32[2,6,32,256]{3,2,1,0:T(8,128)}, f32[2,6,32,256]{3,2,1,0:T(8,128)S(1)}, u32[]{:S(2)}, u32[]{:S(2)}) collective-permute-start(f32[2,6,32,256]{3,2,1,0:T(8,128)} %param.3), channel_id=1, source_target_pairs={{8,0},{16,8},{24,16},{9,1},{17,9},{25,17},{10,2},{18,10},{26,18},{... | collective-permute-start | bytes 1179656 | tf_op jit(solution)/shard_map/ppermute | solution.py:25
  10.4 0.9 copy-start.1
  29.4 13.9 %collective-permute-start.2 = (f32[2,6,32,256]{3,2,1,0:T(8,128)S(1)}, f32[2,6,32,256]{3,2,1,0:T(8,128)S(1)}, u32[]{:S(2)}, u32[]{:S(2)}) collective-permute-start(f32[2,6,32,256]{3,2,1,0:T(8,128)S(1)} %get-tuple-element.2), channel_id=1, source_target_pairs={{8,0},{16,8},{24,16},{9,1},{17,9},{25,17},{10,2},{18,10},{26,18},{... | collective-permute-start | bytes 1179656 | tf_op jit(solution)/shard_map/ppermute | solution.py:25
  30.7 12.6 %collective-permute-start.3 = (f32[2,6,32,256]{3,2,1,0:T(8,128)S(1)}, f32[2,6,32,256]{3,2,1,0:T(8,128)S(1)}, u32[]{:S(2)}, u32[]{:S(2)}) collective-permute-start(f32[2,6,32,256]{3,2,1,0:T(8,128)S(1)} %get-tuple-element.2), channel_id=1, source_target_pairs={{0,8},{8,16},{16,24},{1,9},{9,17},{17,25},{2,10},{10,18},{18,26},{... | collective-permute-start | bytes 1179656 | tf_op jit(solution)/shard_map/ppermute | solution.py:23
  47.1 17.8 %collective-permute-start.4 = (f32[2,6,32,256]{3,2,1,0:T(8,128)S(1)}, f32[2,6,32,256]{3,2,1,0:T(8,128)S(1)}, u32[]{:S(2)}, u32[]{:S(2)}) collective-permute-start(f32[2,6,32,256]{3,2,1,0:T(8,128)S(1)} %fusion.58), channel_id=1, source_target_pairs={{8,0},{16,8},{24,16},{9,1},{17,9},{25,17},{10,2},{18,10},{26,18},{... | collective-permute-start | bytes 1179656 | tf_op jit(solution)/shard_map/ppermute | solution.py:25
  48.4 16.6 %collective-permute-start.5 = (f32[2,6,32,256]{3,2,1,0:T(8,128)S(1)}, f32[2,6,32,256]{3,2,1,0:T(8,128)S(1)}, u32[]{:S(2)}, u32[]{:S(2)}) collective-permute-start(f32[2,6,32,256]{3,2,1,0:T(8,128)S(1)} %fusion.58), channel_id=1, source_target_pairs={{0,8},{8,16},{16,24},{1,9},{9,17},{17,25},{2,10},{10,18},{18,26},{... | collective-permute-start | bytes 1179656 | tf_op jit(solution)/shard_map/ppermute | solution.py:23
  67.5 0.7 copy-start.2

commit v2 on v1

v2 whole, which is shorter than its diff:
```python
import functools

import jax
import jax.numpy as jnp
from jax import lax
from jax.experimental import pallas as pl
from jax.experimental.pallas import tpu as pltpu
from jax.sharding import PartitionSpec as P

DEG_MAX = 3


CENTER_COEF = -5369.0 / 1800.0
STENCIL = (12.0 / 7.0, -15.0 / 56.0, 10.0 / 189.0, -1.0 / 112.0, 2.0 / 1925.0, -1.0 / 16632.0)
SHIFT_C = 8.5
HALF_W = 4.5
RADIUS = len(STENCIL)


def shifted(x, k):
    count = lax.axis_size("dom")
    pairs = [(i, i + k) for i in range(count) if 0 <= i + k < count]
    if not pairs:
        return jnp.zeros_like(x)
    return lax.ppermute(x, "dom", pairs)


def wide_halo(orbitals, potential, orb_halo, pot_halo):
    slab = orbitals.shape[1]
    block_orbs = orbitals.shape[0]
    lefts, rights, pot_lefts, pot_rights = [], [], [], []
    k = 1
    while slab * (k - 1) < orb_halo:
        count = min(slab, orb_halo - slab * (k - 1))
        with_pot = slab * (k - 1) < pot_halo
        tail = orbitals[:, slab - count :]
        head = orbitals[:, :count]
        if with_pot:
            tail = jnp.concatenate([tail, potential[None, slab - count :]], axis=0)
            head = jnp.concatenate([head, potential[None, :count]], axis=0)
        got_left = shifted(tail, k)
        got_right = shifted(head, -k)
        lefts.insert(0, got_left[:block_orbs])
        rights.append(got_right[:block_orbs])
        if with_pot:
            pot_lefts.insert(0, got_left[block_orbs])
            pot_rights.append(got_right[block_orbs])
        else:
            pot_lefts.insert(0, jnp.zeros((count,) + potential.shape[1:], potential.dtype))
            pot_rights.append(jnp.zeros((count,) + potential.shape[1:], potential.dtype))
        k += 1
    cells = jnp.concatenate(lefts + [orbitals] + rights, axis=1)
    pot = jnp.concatenate(pot_lefts + [potential] + pot_rights, axis=0)
    return cells, pot


def filter_kernel(first_ref, deg_ref, cells_ref, pot_ref, out_ref, *iter_refs, grid_planes):
    block_orbs, _, ny, nz = cells_ref.shape
    slab = out_ref.shape[1]
    first = first_ref[0]
    degree = deg_ref[0]
    sources = (cells_ref,) + iter_refs

    def plane_value(order, b, p):
        source = sources[order - 1]
        field = source[b, RADIUS + p]
        laplace = (3.0 * CENTER_COEF) * field
        for offset, weight in enumerate(STENCIL, 1):
            beside_all = source[b, RADIUS + p + offset] + source[b, RADIUS + p - offset]
            beside_all = beside_all + pltpu.roll(field, offset, 0) + pltpu.roll(field, ny - offset, 0)
            beside_all = beside_all + pltpu.roll(field, offset, 1) + pltpu.roll(field, nz - offset, 1)
            laplace = laplace + weight * beside_all
        margin = (DEG_MAX - order) * RADIUS
        applied = -0.5 * laplace + pot_ref[order * RADIUS + p] * field
        if order == 1:
            return (applied - SHIFT_C * field) / HALF_W
        before = sources[order - 2][b, 2 * RADIUS + p]
        return 2.0 * (applied - SHIFT_C * field) / HALF_W - before

    for order in range(1, DEG_MAX):
        margin = (DEG_MAX - order) * RADIUS
        dest = iter_refs[order - 1]
        planes = slab + 2 * margin
        for b in range(block_orbs):
            def body(p, carry, order=order, b=b, dest=dest, margin=margin):
                value = plane_value(order, b, p)
                plane = first + order * RADIUS + p
                keep = jnp.full((ny, nz), plane, jnp.int32)
                keep = (keep >= 0) & (keep < grid_planes)
                dest[b, p] = jnp.where(keep, value, 0.0)
                return carry
            lax.fori_loop(0, planes, body, 0)

    for b in range(block_orbs):
        def last(p, carry, b=b):
            value = plane_value(DEG_MAX, b, p)
            levels = jnp.full((ny, nz), degree, jnp.int32)
            picked = iter_refs[0][b, (DEG_MAX - 1) * RADIUS + p]
            for order in range(2, DEG_MAX):
                picked = jnp.where(levels >= order, iter_refs[order - 1][b, (DEG_MAX - order) * RADIUS + p], picked)
            picked = jnp.where(levels >= DEG_MAX, value, picked)
            out_ref[b, p] = picked.astype(out_ref.dtype)
            return carry
        lax.fori_loop(0, slab, last, 0)


def chebyshev_filter(cells, pot, first, degree, grid_planes):
    block_orbs, planes, ny, nz = cells.shape
    slab = planes - 2 * DEG_MAX * RADIUS
    smem = pl.BlockSpec(memory_space=pltpu.SMEM)
    vmem = pl.BlockSpec(memory_space=pltpu.VMEM)
    return pl.pallas_call(
        functools.partial(filter_kernel, grid_planes=grid_planes),
        out_shape=jax.ShapeDtypeStruct((block_orbs, slab, ny, nz), jnp.bfloat16),
        in_specs=[smem, smem, vmem, vmem],
        out_specs=vmem,
        scratch_shapes=[
            pltpu.VMEM((block_orbs, slab + 2 * (DEG_MAX - order) * RADIUS, ny, nz), jnp.float32)
            for order in range(1, DEG_MAX)
        ],
    )(first, degree, cells, pot)


def inner_rows(left, right):
    return lax.dot_general(
        left, right, (((1,), (1,)), ((), ())), preferred_element_type=jnp.float32
    )


def per_device(orbitals, potential, degrees):
    block_orbs, slab = orbitals.shape[0], orbitals.shape[1]
    n_orb, n_dom = lax.axis_size("orb"), lax.axis_size("dom")
    grid_planes = slab * n_dom
    start = lax.axis_index("dom") * slab
    reach = DEG_MAX * RADIUS
    cells, pot = wide_halo(orbitals, potential, reach, reach - RADIUS)
    first = (start - reach).astype(jnp.int32).reshape(1)
    filtered = chebyshev_filter(cells, pot, first, degrees.astype(jnp.int32), grid_planes)
    cell_count = orbitals.shape[1] * orbitals.shape[2] * orbitals.shape[3]
    total_cells = float(cell_count * n_dom)
    flattened = filtered.reshape(block_orbs, cell_count)
    mixed = lax.all_to_all(flattened, "orb", split_axis=1, concat_axis=0, tiled=True)
    partial_gram = inner_rows(mixed, mixed)
    rows = partial_gram.reshape(n_orb, 1, block_orbs, -1)
    sends = jnp.broadcast_to(rows, (n_orb, n_dom) + rows.shape[2:]).reshape((n_orb * n_dom,) + rows.shape[2:])
    gathered = lax.all_to_all(sends, ("orb", "dom"), split_axis=0, concat_axis=0, tiled=True)
    correlation = gathered.sum(axis=0) / total_cells
    return (filtered, correlation)


def solution(mesh):
    placed = (P("orb", "dom", None, None), P("dom", None, None), P("orb"))
    return jax.shard_map(
        per_device,
        mesh=mesh,
        in_specs=placed,
        out_specs=(P("orb", "dom", None, None), P("orb", None)),
        check_vma=False,
    )
```

time: 100 us -> 96.9 us (0.969)
  Pallas kernels: 0 us -> 22.4 us
  waiting for transfers between devices: 27.4 us -> 14.8 us
  starting transfers between devices: 22 us -> 14.5 us
  other arithmetic: 8.04 us -> 2.63 us
  blocking collectives: 30.4 us -> 27 us
  local copies, waits for them, and re-layouts: 9.99 us -> 13.2 us
    pallas_call x0 -> x1, Pallas kernels: none -> 22.4 us  [chebyshev_filter(): pl.pallas_call(functools.partial(filter_kernel, grid_planes=grid_planes),...]
    ppermute x6, waiting for transfers between devices: 27.4 us -> 14.8 us  [shifted(): return lax.ppermute(x, 'dom', pairs)]
    unnamed x8 -> x22, local copies, waits for them, and re-layouts: 1.34 us -> 11.5 us
    slice x72 -> x0, local copies, waits for them, and re-layouts: 7.94 us -> none  [the longest x24 3.52 us: hamiltonian(): jnp.roll(field, offset, 3)]
    ppermute x6, starting transfers between devices: 22 us -> 14.5 us  [shifted(): return lax.ppermute(x, 'dom', pairs)]
    all_to_all x1, blocking collectives: 17.4 us -> 14 us  [per_device(): lax.all_to_all(sends, ('orb', 'dom'), split_axis=0, concat_axis=0, tiled=...]
    convert_element_type x1 -> x0, other arithmetic: 2.52 us -> none  [per_device(): filtered = picked.astype(jnp.bfloat16)]
    div x1 -> x0, other arithmetic: 2.45 us -> none  [per_device(): first = (hamiltonian(orbitals, potential) - SHIFT_C * orbitals) / HALF_W]
  transfers between devices with their start and end apart: 6 -> 6, of which waited for: 4 -> 3; matrix products, arithmetic and copies ran while one was open for 5% -> 10% of each run, Pallas kernels for 0% -> 0%
where the time goes in v2:
time: 96.9 us; the launch traced here: 96.2 us
  blocking collectives  27 us (28%)
  Pallas kernels  22.4 us (23%)
  waiting for transfers between devices  14.8 us (15%)
  starting transfers between devices  14.5 us (15%)
  local copies, waits for them, and re-layouts  13.2 us (14%)
  other arithmetic  2.63 us (3%)
  between operations  1.53 us (2%)
    pallas_call x1, Pallas kernels, chebyshev_filter(): pl.pallas_call(functools.partial(filter_kernel, grid_planes=grid_planes),...  22.4 us
    ppermute x6, waiting for transfers between devices, shifted(): return lax.ppermute(x, 'dom', pairs)  14.8 us
    ppermute x6, starting transfers between devices, shifted(): return lax.ppermute(x, 'dom', pairs)  14.5 us
    all_to_all x1, blocking collectives, per_device(): lax.all_to_all(sends, ('orb', 'dom'), split_axis=0, concat_axis=0, tiled=...  14 us
    all_to_all x1, blocking collectives, per_device(): lax.all_to_all(flattened, 'orb', split_axis=1, concat_axis=0, tiled=True)  13 us
    unnamed x22, local copies, waits for them, and re-layouts  11.5 us
    concatenate x1, other arithmetic, wide_halo(): tail = jnp.concatenate([tail, potential[None, slab - count:]], axis=0)  2.02 us
  transfers between devices with their start and end apart: 6, of which 3 were waited for; matrix products, arithmetic and copies ran while one was open for 10% of the time, Pallas kernels for 0%

profile of v2, /device:TPU:0, one launch (start us, length us, event | category | flops | bytes accessed | tf_op | source)
XLA Modules:
  0.0 96.2 jit_solution(11897810392849851402)
XLA Ops:
  0.6 0.0 copy-start.2
  0.7 2.0 %pad_maximum_fusion = f32[3,6,32,256]{3,2,1,0:T(8,128)} fusion(f32[1,6,32,256]{3,2,1,0:T(8,128)} %bitcast.26, f32[2,6,32,256]{3,2,1,0:T(8,128)} %param.3), kind=kLoop, calls=%fused_computation | loop fusion | flops 147456 | bytes 1179648 | tf_op jit(solution)/shard_map/concatenate | solution.py:39
  2.7 5.7 %collective-permute-start.1 = (f32[3,6,32,256]{3,2,1,0:T(8,128)}, f32[3,6,32,256]{3,2,1,0:T(8,128)}, u32[]{:S(2)}, u32[]{:S(2)}) collective-permute-start(f32[3,6,32,256]{3,2,1,0:T(8,128)} %pad_maximum_fusion), channel_id=1, source_target_pairs={{0,16},{8,24},{1,17},{9,25},{2,18},{10,26},{3,19},{11,27},{4,20},{... | collective-permute-start | bytes 1769480 | tf_op jit(solution)/shard_map/ppermute | solution.py:25
  8.4 1.4 %collective-permute-start = (f32[2,6,32,256]{3,2,1,0:T(8,128)}, f32[2,6,32,256]{3,2,1,0:T(8,128)S(1)}, u32[]{:S(2)}, u32[]{:S(2)}) collective-permute-start(f32[2,6,32,256]{3,2,1,0:T(8,128)} %param.3), channel_id=1, source_target_pairs={{0,24},{1,25},{2,26},{3,27},{4,28},{5,29},{6,30},{7,31}} | collective-permute-start | bytes 1179656 | tf_op jit(solution)/shard_map/ppermute | solution.py:25
  9.8 3.5 %collective-permute-start.2 = (f32[3,6,32,256]{3,2,1,0:T(8,128)}, f32[3,6,32,256]{3,2,1,0:T(8,128)}, u32[]{:S(2)}, u32[]{:S(2)}) collective-permute-start(f32[3,6,32,256]{3,2,1,0:T(8,128)} %pad_maximum_fusion), channel_id=1, source_target_pairs={{0,8},{8,16},{16,24},{1,9},{9,17},{17,25},{2,10},{10,18},{18,26},{... | collective-permute-start | bytes 1769480 | tf_op jit(solution)/shard_map/ppermute | solution.py:25
  13.3 1.3 %collective-permute-start.3 = (f32[3,6,32,256]{3,2,1,0:T(8,128)}, f32[3,6,32,256]{3,2,1,0:T(8,128)}, u32[]{:S(2)}, u32[]{:S(2)}) collective-permute-start(f32[3,6,32,256]{3,2,1,0:T(8,128)} %pad_maximum_fusion), channel_id=1, source_target_pairs={{8,0},{16,8},{24,16},{9,1},{17,9},{25,17},{10,2},{18,10},{26,18},{... | collective-permute-start | bytes 1769480 | tf_op jit(solution)/shard_map/ppermute | solution.py:25
  14.6 1.3 %collective-permute-start.4 = (f32[3,6,32,256]{3,2,1,0:T(8,128)}, f32[3,6,32,256]{3,2,1,0:T(8,128)}, u32[]{:S(2)}, u32[]{:S(2)}) collective-permute-start(f32[3,6,32,256]{3,2,1,0:T(8,128)} %pad_maximum_fusion), channel_id=1, source_target_pairs={{16,0},{24,8},{17,1},{25,9},{18,2},{26,10},{19,3},{27,11},{20,4},{... | collective-permute-start | bytes 1769480 | tf_op jit(solution)/shard_map/ppermute | solution.py:25
  16.6 3.0 %collective-permute-done = f32[2,6,32,256]{3,2,1,0:T(8,128)S(1)} collective-permute-done((f32[2,6,32,256]{3,2,1,0:T(8,128)}, f32[2,6,32,256]{3,2,1,0:T(8,128)S(1)}, u32[]{:S(2)}, u32[]{:S(2)}) %collective-permute-start) | collective-permute-done | bytes 393248 | tf_op jit(solution)/shard_map/ppermute | solution.py:25
  19.6 0.8 copy-done.4
  20.4 1.3 %collective-permute-start.5 = (f32[2,6,32,256]{3,2,1,0:T(8,128)}, f32[2,6,32,256]{3,2,1,0:T(8,128)S(1)}, u32[]{:S(2)}, u32[]{:S(2)}) collective-permute-start(f32[2,6,32,256]{3,2,1,0:T(8,128)} %param.3), channel_id=1, source_target_pairs={{24,0},{25,1},{26,2},{27,3},{28,4},{29,5},{30,6},{31,7}} | collective-permute-start | bytes 1179656 | tf_op jit(solution)/shard_map/ppermute | solution.py:25
  21.6 1.0 %constant_dynamic-update-slice_fusion.2 = f32[2,42,32,256]{3,2,1,0:T(8,128)S(1)} fusion(f32[2,6,32,256]{3,2,1,0:T(8,128)} %copy-done.4), kind=kLoop, calls=%fused_computation.18 | loop fusion | bytes 786432
  22.7 10.4 %collective-permute-done.1 = f32[3,6,32,256]{3,2,1,0:T(8,128)} collective-permute-done((f32[3,6,32,256]{3,2,1,0:T(8,128)}, f32[3,6,32,256]{3,2,1,0:T(8,128)}, u32[]{:S(2)}, u32[]{:S(2)}) %collective-permute-start.1) | collective-permute-done | bytes 589856 | tf_op jit(solution)/shard_map/ppermute | solution.py:25
  33.1 1.0 %slice_dynamic-update-slice_fusion.3 = f32[2,42,32,256]{3,2,1,0:T(8,128)S(1)} fusion(f32[2,42,32,256]{3,2,1,0:T(8,128)S(1)} %constant_dynamic-update-slice_fusion.2, f32[3,6,32,256]{3,2,1,0:T(8,128)} %collective-permute-done.1), kind=kLoop, calls=%fused_computation.4 | loop fusion | bytes 786432
  34.1 1.0 %slice_dynamic-update-slice_fusion.2 = f32[2,42,32,256]{3,2,1,0:T(8,128)S(1)} fusion(f32[2,42,32,256]{3,2,1,0:T(8,128)S(1)} %slice_dynamic-update-slice_fusion.3, f32[3,6,32,256]{3,2,1,0:T(8,128)} %collective-permute-done.2), kind=kLoop, calls=%fused_computation.3 | loop fusion | bytes 786432
  35.2 0.9 fusion.3
  36.2 0.9 fusion.2
  37.1 1.4 %collective-permute-done.3 = f32[3,6,32,256]{3,2,1,0:T(8,128)} collective-permute-done((f32[3,6,32,256]{3,2,1,0:T(8,128)}, f32[3,6,32,256]{3,2,1,0:T(8,128)}, u32[]{:S(2)}, u32[]{:S(2)}) %collective-permute-start.3) | collective-permute-done | bytes 589856 | tf_op jit(solution)/shard_map/ppermute | solution.py:25
  38.5 0.9 fusion.1
  39.5 1.0 %slice_dynamic-update-slice_fusion.1 = f32[2,42,32,256]{3,2,1,0:T(8,128)S(1)} fusion(f32[2,42,32,256]{3,2,1,0:T(8,128)S(1)} %constant_dynamic-update-slice_fusion.1, f32[3,6,32,256]{3,2,1,0:T(8,128)} %collective-permute-done.3), kind=kLoop, calls=%fused_computation.2 | loop fusion | bytes 786432
  40.5 0.9 fusion
  41.5 1.3 %slice_dynamic-update-slice_fusion = f32[2,42,32,256]{3,2,1,0:T(8,128)S(1)} fusion(f32[2,42,32,256]{3,2,1,0:T(8,128)S(1)} %slice_dynamic-update-slice_fusion.1, f32[3,6,32,256]{3,2,1,0:T(8,128)} %collective-permute-done.4), kind=kLoop, calls=%fused_computation.1 | loop fusion | bytes 786432
  42.9 1.5 %copy-done = f32[2,42,32,256]{3,2,1,0:T(8,128)} copy-done((f32[2,42,32,256]{3,2,1,0:T(8,128)}, f32[2,42,32,256]{3,2,1,0:T(8,128)S(1)}, u32[]{:S(2)}) %copy-start) | copy-done | bytes 2752536
  44.4 22.4 %shard_map.50 = bf16[2,6,32,256]{3,2,1,0:T(8,128)(2,1)} custom-call(s32[1]{0:T(128)} %bitcast.first_ref, s32[1]{0:T(128)S(6)} %copy.40.deg_ref, f32[2,42,32,256]{3,2,1,0:T(8,128)} %copy-done, f32[42,32,256]{2,1,0:T(8,128)} %copy-done.1), custom_call_target="tpu_custom_call" | custom-call | tf_op jit(solution)/shard_map/pallas_call | solution.py:112
  66.8 1.0 %all_to_all.17 = bf16[2,8,6144]{2,1,0:T(8,128)(2,1)S(1)} reshape(bf16[2,6,32,256]{3,2,1,0:T(8,128)(2,1)} %shard_map.50) | data formatting | bytes 393216 | tf_op jit(solution)/shard_map/all_to_all | solution.py:142
  67.8 0.2 copy.19
  68.0 13.0 %all_to_all.24 = bf16[2,8,6144]{2,0,1:T(2,128)(2,1)S(1)} all-to-all(bf16[2,8,6144]{2,0,1:T(2,128)(2,1)S(1)} %copy.19), channel_id=1, replica_groups=mesh['dom'=4,'orb'=8] {'orb'}, dimensions={1} | all-to-all | bytes 393216 | tf_op jit(solution)/shard_map/all_to_all | solution.py:142
  81.0 0.1 copy.27
  81.1 0.2 copy.21
  81.3 0.1 reshape.24
  81.4 0.2 fusion.4
  81.6 14.0 %all_to_all.25 = f32[32,2,16]{2,1,0:T(2,128)S(1)} all-to-all(f32[32,2,16]{2,1,0:T(2,128)S(1)} %copy.22), channel_id=1, replica_groups=mesh['dom'=4,'orb'=8] {'orb','dom'}, dimensions={0} | all-to-all | bytes 8192 | tf_op jit(solution)/shard_map/all_to_all | solution.py:146
  95.7 0.6 broadcast_multiply_fusion
  (18 shorter events, 0.2 us)
Async XLA Ops:
  0.6 36.5 %copy-start.3 = (f32[6,32,256]{2,1,0:T(8,128)S(1)}, f32[6,32,256]{2,1,0:T(8,128)}, u32[]{:S(2)}) copy-start(f32[6,32,256]{2,1,0:T(8,128)} %param.4) | copy-start | bytes 589828
  0.6 34.5 %copy-start.2 = (f32[2,6,32,256]{3,2,1,0:T(8,128)S(1)}, f32[2,6,32,256]{3,2,1,0:T(8,128)}, u32[]{:S(2)}) copy-start(f32[2,6,32,256]{3,2,1,0:T(8,128)} %param.3) | copy-start | bytes 1179652
  2.7 30.4 %collective-permute-start.1 = (f32[3,6,32,256]{3,2,1,0:T(8,128)}, f32[3,6,32,256]{3,2,1,0:T(8,128)}, u32[]{:S(2)}, u32[]{:S(2)}) collective-permute-start(f32[3,6,32,256]{3,2,1,0:T(8,128)} %pad_maximum_fusion), channel_id=1, source_target_pairs={{0,16},{8,24},{1,17},{9,25},{2,18},{10,26},{3,19},{11,27},{4,20},{... | collective-permute-start | bytes 1769480 | tf_op jit(solution)/shard_map/ppermute | solution.py:25
  8.4 11.2 %collective-permute-start = (f32[2,6,32,256]{3,2,1,0:T(8,128)}, f32[2,6,32,256]{3,2,1,0:T(8,128)S(1)}, u32[]{:S(2)}, u32[]{:S(2)}) collective-permute-start(f32[2,6,32,256]{3,2,1,0:T(8,128)} %param.3), channel_id=1, source_target_pairs={{0,24},{1,25},{2,26},{3,27},{4,28},{5,29},{6,30},{7,31}} | collective-permute-start | bytes 1179656 | tf_op jit(solution)/shard_map/ppermute | solution.py:25
  9.8 24.3 %collective-permute-start.2 = (f32[3,6,32,256]{3,2,1,0:T(8,128)}, f32[3,6,32,256]{3,2,1,0:T(8,128)}, u32[]{:S(2)}, u32[]{:S(2)}) collective-permute-start(f32[3,6,32,256]{3,2,1,0:T(8,128)} %pad_maximum_fusion), channel_id=1, source_target_pairs={{0,8},{8,16},{16,24},{1,9},{9,17},{17,25},{2,10},{10,18},{18,26},{... | collective-permute-start | bytes 1769480 | tf_op jit(solution)/shard_map/ppermute | solution.py:25
  13.3 25.2 %collective-permute-start.3 = (f32[3,6,32,256]{3,2,1,0:T(8,128)}, f32[3,6,32,256]{3,2,1,0:T(8,128)}, u32[]{:S(2)}, u32[]{:S(2)}) collective-permute-start(f32[3,6,32,256]{3,2,1,0:T(8,128)} %pad_maximum_fusion), channel_id=1, source_target_pairs={{8,0},{16,8},{24,16},{9,1},{17,9},{25,17},{10,2},{18,10},{26,18},{... | collective-permute-start | bytes 1769480 | tf_op jit(solution)/shard_map/ppermute | solution.py:25
  14.6 25.9 %collective-permute-start.4 = (f32[3,6,32,256]{3,2,1,0:T(8,128)}, f32[3,6,32,256]{3,2,1,0:T(8,128)}, u32[]{:S(2)}, u32[]{:S(2)}) collective-permute-start(f32[3,6,32,256]{3,2,1,0:T(8,128)} %pad_maximum_fusion), channel_id=1, source_target_pairs={{16,0},{24,8},{17,1},{25,9},{18,2},{26,10},{19,3},{27,11},{20,4},{... | collective-permute-start | bytes 1769480 | tf_op jit(solution)/shard_map/ppermute | solution.py:25
  19.6 0.8 copy-start.4
  20.4 22.5 %collective-permute-start.5 = (f32[2,6,32,256]{3,2,1,0:T(8,128)}, f32[2,6,32,256]{3,2,1,0:T(8,128)S(1)}, u32[]{:S(2)}, u32[]{:S(2)}) collective-permute-start(f32[2,6,32,256]{3,2,1,0:T(8,128)} %param.3), channel_id=1, source_target_pairs={{24,0},{25,1},{26,2},{27,3},{28,4},{29,5},{30,6},{31,7}} | collective-permute-start | bytes 1179656 | tf_op jit(solution)/shard_map/ppermute | solution.py:25
  41.5 1.4 %copy-start.1 = (f32[42,32,256]{2,1,0:T(8,128)}, f32[42,32,256]{2,1,0:T(8,128)S(1)}, u32[]{:S(2)}) copy-start(f32[42,32,256]{2,1,0:T(8,128)S(1)} %broadcast_dynamic-update-slice_fusion.1.pot_ref) | copy-start | bytes 4128772
  42.9 1.5 %copy-start = (f32[2,42,32,256]{3,2,1,0:T(8,128)}, f32[2,42,32,256]{3,2,1,0:T(8,128)S(1)}, u32[]{:S(2)}) copy-start(f32[2,42,32,256]{3,2,1,0:T(8,128)S(1)} %constant_dynamic-update-slice_fusion.cells_ref) | copy-start | bytes 8257540

commit v3 on v2

--- a/solution.py
+++ b/solution.py
@@ -25,41 +25,68 @@
     return lax.ppermute(x, "dom", pairs)
 
 
-def wide_halo(orbitals, potential, orb_halo, pot_halo):
-    slab = orbitals.shape[1]
-    block_orbs = orbitals.shape[0]
-    lefts, rights, pot_lefts, pot_rights = [], [], [], []
+def halo_pieces(values, axis, halo):
+    slab = values.shape[axis]
+    below, above = [], []
     k = 1
-    while slab * (k - 1) < orb_halo:
-        count = min(slab, orb_halo - slab * (k - 1))
-        with_pot = slab * (k - 1) < pot_halo
-        tail = orbitals[:, slab - count :]
-        head = orbitals[:, :count]
-        if with_pot:
-            tail = jnp.concatenate([tail, potential[None, slab - count :]], axis=0)
-            head = jnp.concatenate([head, potential[None, :count]], axis=0)
-        got_left = shifted(tail, k)
-        got_right = shifted(head, -k)
-        lefts.insert(0, got_left[:block_orbs])
-        rights.append(got_right[:block_orbs])
-        if with_pot:
-            pot_lefts.insert(0, got_left[block_orbs])
-            pot_rights.append(got_right[block_orbs])
-        else:
-            pot_lefts.insert(0, jnp.zeros((count,) + potential.shape[1:], potential.dtype))
-            pot_rights.append(jnp.zeros((count,) + potential.shape[1:], potential.dtype))
+    while slab * (k - 1) < halo:
+        count = min(slab, halo - slab * (k - 1))
+        tail = lax.slice_in_dim(values, slab - count, slab, axis=axis)
+        head = lax.slice_in_dim(values, 0, count, axis=axis)
+        below.append(shifted(tail, k))
+        above.append(shifted(head, -k))
         k += 1
-    cells = jnp.concatenate(lefts + [orbitals] + rights, axis=1)
-    pot = jnp.concatenate(pot_lefts + [potential] + pot_rights, axis=0)
-    return cells, pot
+    return below, above
 
 
-def filter_kernel(first_ref, deg_ref, cells_ref, pot_ref, out_ref, *iter_refs, grid_planes):
+def filter_kernel(first_ref, deg_ref, *refs, n_orb_pieces, n_pot_pieces, grid_planes):
+    n_in = 2 + 2 * n_orb_pieces + 2 * n_pot_pieces
+    ins = refs[:n_in]
+    out_ref = refs[n_in]
+    cells_ref, pot_ref, sems = refs[n_in + 1], refs[n_in + 2], refs[n_in + 3]
+    iter_refs = refs[n_in + 4 :]
+    orb_in, pot_in = ins[0], ins[1]
+    orb_below = ins[2 : 2 + n_orb_pieces]
+    orb_above = ins[2 + n_orb_pieces : 2 + 2 * n_orb_pieces]
+    pot_below = ins[2 + 2 * n_orb_pieces : 2 + 2 * n_orb_pieces + n_pot_pieces]
+    pot_above = ins[2 + 2 * n_orb_pieces + n_pot_pieces :]
     block_orbs, _, ny, nz = cells_ref.shape
     slab = out_ref.shape[1]
     first = first_ref[0]
     degree = deg_ref[0]
-    sources = (cells_ref,) + iter_refs
+
+    copies = []
+
+    def place(src, dst_ref, lo, axis):
+        count = src.shape[axis]
+        if axis == 1:
+            dst = dst_ref.at[:, pl.ds(lo, count)]
+        else:
+            dst = dst_ref.at[pl.ds(lo, count)]
+        copy = pltpu.make_async_copy(src, dst, sems.at[len(copies)])
+        copy.start()
+        copies.append(copy)
+
+    reach = DEG_MAX * RADIUS
+    place(orb_in, cells_ref, reach, 1)
+    lo, hi = reach, reach + slab
+    for piece_below, piece_above in zip(orb_below, orb_above):
+        lo -= piece_below.shape[1]
+        place(piece_below, cells_ref, lo, 1)
+        place(piece_above, cells_ref, hi, 1)
+        hi += piece_above.shape[1]
+    pot_reach = reach - RADIUS
+    place(pot_in, pot_ref, pot_reach, 0)
+    lo, hi = pot_reach, pot_reach + slab
+    for piece_below, piece_above in zip(pot_below, pot_above):
+        lo -= piece_below.shape[0]
+        place(piece_below, pot_ref, lo, 0)
+        place(piece_above, pot_ref, hi, 0)
+        hi += piece_above.shape[0]
+    for copy in copies:
+        copy.wait()
+
+    sources = (cells_ref,) + tuple(iter_refs)
 
     def plane_value(order, b, p):
         source = sources[order - 1]
@@ -70,8 +97,7 @@
             beside_all = beside_all + pltpu.roll(field, offset, 0) + pltpu.roll(field, ny - offset, 0)
             beside_all = beside_all + pltpu.roll(field, offset, 1) + pltpu.roll(field, nz - offset, 1)
             laplace = laplace + weight * beside_all
-        margin = (DEG_MAX - order) * RADIUS
-        applied = -0.5 * laplace + pot_ref[order * RADIUS + p] * field
+        applied = -0.5 * laplace + pot_ref[(order - 1) * RADIUS + p] * field
         if order == 1:
             return (applied - SHIFT_C * field) / HALF_W
         before = sources[order - 2][b, 2 * RADIUS + p]
@@ -82,7 +108,7 @@
         dest = iter_refs[order - 1]
         planes = slab + 2 * margin
         for b in range(block_orbs):
-            def body(p, carry, order=order, b=b, dest=dest, margin=margin):
+            def body(p, carry, order=order, b=b, dest=dest):
                 value = plane_value(order, b, p)
                 plane = first + order * RADIUS + p
                 keep = jnp.full((ny, nz), plane, jnp.int32)
@@ -104,21 +130,36 @@
         lax.fori_loop(0, slab, last, 0)
 
 
-def chebyshev_filter(cells, pot, first, degree, grid_planes):
-    block_orbs, planes, ny, nz = cells.shape
-    slab = planes - 2 * DEG_MAX * RADIUS
+def chebyshev_filter(orbitals, potential, first, degree, grid_planes):
+    block_orbs, slab, ny, nz = orbitals.shape
+    reach = DEG_MAX * RADIUS
+    orb_below, orb_above = halo_pieces(orbitals, 1, reach)
+    pot_below, pot_above = halo_pieces(potential, 0, reach - RADIUS)
+    operands = [orbitals, potential] + orb_below + orb_above + pot_below + pot_above
     smem = pl.BlockSpec(memory_space=pltpu.SMEM)
+    hbm = pl.BlockSpec(memory_space=pl.ANY)
     vmem = pl.BlockSpec(memory_space=pltpu.VMEM)
+    n_copies = len(operands)
     return pl.pallas_call(
-        functools.partial(filter_kernel, grid_planes=grid_planes),
+        functools.partial(
+            filter_kernel,
+            n_orb_pieces=len(orb_below),
+            n_pot_pieces=len(pot_below),
+            grid_planes=grid_planes,
+        ),
         out_shape=jax.ShapeDtypeStruct((block_orbs, slab, ny, nz), jnp.bfloat16),
-        in_specs=[smem, smem, vmem, vmem],
+        in_specs=[smem, smem] + [hbm] * n_copies,
         out_specs=vmem,
         scratch_shapes=[
+            pltpu.VMEM((block_orbs, slab + 2 * reach, ny, nz), jnp.float32),
+            pltpu.VMEM((slab + 2 * (reach - RADIUS), ny, nz), jnp.float32),
+            pltpu.SemaphoreType.DMA((n_copies,)),
+        ]
+        + [
             pltpu.VMEM((block_orbs, slab + 2 * (DEG_MAX - order) * RADIUS, ny, nz), jnp.float32)
             for order in range(1, DEG_MAX)
         ],
-    )(first, degree, cells, pot)
+    )(first, degree, *operands)
 
 
 def inner_rows(left, right):
@@ -132,10 +173,8 @@
     n_orb, n_dom = lax.axis_size("orb"), lax.axis_size("dom")
     grid_planes = slab * n_dom
     start = lax.axis_index("dom") * slab
-    reach = DEG_MAX * RADIUS
-    cells, pot = wide_halo(orbitals, potential, reach, reach - RADIUS)
-    first = (start - reach).astype(jnp.int32).reshape(1)
-    filtered = chebyshev_filter(cells, pot, first, degrees.astype(jnp.int32), grid_planes)
+    first = (start - DEG_MAX * RADIUS).astype(jnp.int32).reshape(1)
+    filtered = chebyshev_filter(orbitals, potential, first, degrees.astype(jnp.int32), grid_planes)
     cell_count = orbitals.shape[1] * orbitals.shape[2] * orbitals.shape[3]
     total_cells = float(cell_count * n_dom)
     flattened = filtered.reshape(block_orbs, cell_count)

time: 96.9 us -> 96 us (level)
  starting transfers between devices: 14.5 us -> 32.6 us
  local copies, waits for them, and re-layouts: 13.2 us -> 2.32 us
  blocking collectives: 27 us -> 22 us
  other arithmetic: 2.63 us -> 0.61 us
    ppermute x6 -> x10, starting transfers between devices: 14.5 us -> 32.6 us  [shifted(): return lax.ppermute(x, 'dom', pairs)]
    unnamed x22 -> x20, local copies, waits for them, and re-layouts: 11.5 us -> 0.72 us
    all_to_all x1, blocking collectives: 14 us -> 8.99 us  [per_device(): lax.all_to_all(sends, ('orb', 'dom'), split_axis=0, concat_axis=0, tiled=...]
    concatenate x1 -> x0, other arithmetic: 2.02 us -> none  [wide_halo(): tail = jnp.concatenate([tail, potential[None, slab - count:]], axis=0)]
    ppermute x6 -> x10, waiting for transfers between devices: 14.8 us -> 13.9 us  [shifted(): return lax.ppermute(x, 'dom', pairs)]
  transfers between devices with their start and end apart: 6 -> 10, of which waited for: 3 -> 3; matrix products, arithmetic and copies ran while one was open for 10% -> 0% of each run, Pallas kernels for 0% -> 0%
where the time goes in v3:
time: 96 us; the launch traced here: 95.6 us
  starting transfers between devices  32.6 us (34%)
  Pallas kernels  22.3 us (23%)
  blocking collectives  22 us (23%)
  waiting for transfers between devices  13.9 us (14%)
  local copies, waits for them, and re-layouts  2.32 us (2%)
  between operations  1.58 us (2%)
    ppermute x10, starting transfers between devices, shifted(): return lax.ppermute(x, 'dom', pairs)  32.6 us
    pallas_call x1, Pallas kernels, chebyshev_filter(): pl.pallas_call(functools.partial(filter_kernel, n_orb_pieces=len(orb_belo...  22.3 us
    ppermute x10, waiting for transfers between devices, shifted(): return lax.ppermute(x, 'dom', pairs)  13.9 us
    all_to_all x1, blocking collectives, per_device(): lax.all_to_all(flattened, 'orb', split_axis=1, concat_axis=0, tiled=True)  13 us
    all_to_all x1, blocking collectives, per_device(): lax.all_to_all(sends, ('orb', 'dom'), split_axis=0, concat_axis=0, tiled=...  8.99 us
  transfers between devices with their start and end apart: 10, of which 3 were waited for; matrix products, arithmetic and copies ran while one was open for 0% of the time, Pallas kernels for 0%

profile of v3, /device:TPU:0, one launch (start us, length us, event | category | flops | bytes accessed | tf_op | source)
XLA Modules:
  0.0 95.6 jit_solution(10908260071412476989)
XLA Ops:
  0.6 1.3 %collective-permute-start.4 = (f32[2,6,32,256]{3,2,1,0:T(8,128)}, f32[2,6,32,256]{3,2,1,0:T(8,128)S(1)}, u32[]{:S(2)}, u32[]{:S(2)}) collective-permute-start(f32[2,6,32,256]{3,2,1,0:T(8,128)} %refs_0_.1), channel_id=1, source_target_pairs={{16,0},{24,8},{17,1},{25,9},{18,2},{26,10},{19,3},{27,11},{20,4},{... | collective-permute-start | bytes 1179656 | tf_op jit(solution)/shard_map/ppermute | solution.py:25
  1.9 1.3 %collective-permute-start.8 = (f32[6,32,256]{2,1,0:T(8,128)}, f32[6,32,256]{2,1,0:T(8,128)S(1)}, u32[]{:S(2)}, u32[]{:S(2)}) collective-permute-start(f32[6,32,256]{2,1,0:T(8,128)} %refs_1_.1), channel_id=1, source_target_pairs={{8,0},{16,8},{24,16},{9,1},{17,9},{25,17},{10,2},{18,10},{26,18},{... | collective-permute-start | bytes 589832 | tf_op jit(solution)/shard_map/ppermute | solution.py:25
  3.2 7.0 %collective-permute-start.7 = (f32[6,32,256]{2,1,0:T(8,128)}, f32[6,32,256]{2,1,0:T(8,128)S(1)}, u32[]{:S(2)}, u32[]{:S(2)}) collective-permute-start(f32[6,32,256]{2,1,0:T(8,128)} %refs_1_.1), channel_id=1, source_target_pairs={{0,16},{8,24},{1,17},{9,25},{2,18},{10,26},{3,19},{11,27},{4,20},{... | collective-permute-start | bytes 589832 | tf_op jit(solution)/shard_map/ppermute | solution.py:25
  10.2 2.5 %collective-permute-start.6 = (f32[6,32,256]{2,1,0:T(8,128)}, f32[6,32,256]{2,1,0:T(8,128)S(1)}, u32[]{:S(2)}, u32[]{:S(2)}) collective-permute-start(f32[6,32,256]{2,1,0:T(8,128)} %refs_1_.1), channel_id=1, source_target_pairs={{0,8},{8,16},{16,24},{1,9},{9,17},{17,25},{2,10},{10,18},{18,26},{... | collective-permute-start | bytes 589832 | tf_op jit(solution)/shard_map/ppermute | solution.py:25
  12.7 1.3 %collective-permute-start.9 = (f32[6,32,256]{2,1,0:T(8,128)}, f32[6,32,256]{2,1,0:T(8,128)S(1)}, u32[]{:S(2)}, u32[]{:S(2)}) collective-permute-start(f32[6,32,256]{2,1,0:T(8,128)} %refs_1_.1), channel_id=1, source_target_pairs={{16,0},{24,8},{17,1},{25,9},{18,2},{26,10},{19,3},{27,11},{20,4},{... | collective-permute-start | bytes 589832 | tf_op jit(solution)/shard_map/ppermute | solution.py:25
  14.0 0.0 collective-permute-done.8.refs_10_
  14.1 1.3 %collective-permute-start.3 = (f32[2,6,32,256]{3,2,1,0:T(8,128)}, f32[2,6,32,256]{3,2,1,0:T(8,128)S(1)}, u32[]{:S(2)}, u32[]{:S(2)}) collective-permute-start(f32[2,6,32,256]{3,2,1,0:T(8,128)} %refs_0_.1), channel_id=1, source_target_pairs={{8,0},{16,8},{24,16},{9,1},{17,9},{25,17},{10,2},{18,10},{26,18},{... | collective-permute-start | bytes 1179656 | tf_op jit(solution)/shard_map/ppermute | solution.py:25
  15.4 3.2 %collective-permute-done.7.refs_9_ = f32[6,32,256]{2,1,0:T(8,128)S(1)} collective-permute-done((f32[6,32,256]{2,1,0:T(8,128)}, f32[6,32,256]{2,1,0:T(8,128)S(1)}, u32[]{:S(2)}, u32[]{:S(2)}) %collective-permute-start.7) | collective-permute-done | bytes 196640 | tf_op jit(solution)/shard_map/ppermute | solution.py:25
  18.6 3.5 %collective-permute-start.2 = (f32[2,6,32,256]{3,2,1,0:T(8,128)}, f32[2,6,32,256]{3,2,1,0:T(8,128)S(1)}, u32[]{:S(2)}, u32[]{:S(2)}) collective-permute-start(f32[2,6,32,256]{3,2,1,0:T(8,128)} %refs_0_.1), channel_id=1, source_target_pairs={{0,24},{1,25},{2,26},{3,27},{4,28},{5,29},{6,30},{7,31}} | collective-permute-start | bytes 1179656 | tf_op jit(solution)/shard_map/ppermute | solution.py:25
  22.1 0.0 collective-permute-done.6.refs_8_
  22.1 1.5 %collective-permute-start.1 = (f32[2,6,32,256]{3,2,1,0:T(8,128)}, f32[2,6,32,256]{3,2,1,0:T(8,128)S(1)}, u32[]{:S(2)}, u32[]{:S(2)}) collective-permute-start(f32[2,6,32,256]{3,2,1,0:T(8,128)} %refs_0_.1), channel_id=1, source_target_pairs={{0,16},{8,24},{1,17},{9,25},{2,18},{10,26},{3,19},{11,27},{4,20},{... | collective-permute-start | bytes 1179656 | tf_op jit(solution)/shard_map/ppermute | solution.py:25
  23.6 0.0 collective-permute-done.9.refs_11_
  23.6 11.7 %collective-permute-start = (f32[2,6,32,256]{3,2,1,0:T(8,128)}, f32[2,6,32,256]{3,2,1,0:T(8,128)S(1)}, u32[]{:S(2)}, u32[]{:S(2)}) collective-permute-start(f32[2,6,32,256]{3,2,1,0:T(8,128)} %refs_0_.1), channel_id=1, source_target_pairs={{0,8},{8,16},{16,24},{1,9},{9,17},{17,25},{2,10},{10,18},{18,26},{... | collective-permute-start | bytes 1179656 | tf_op jit(solution)/shard_map/ppermute | solution.py:25
  35.3 0.0 collective-permute-done.4.refs_6_
  35.3 0.0 copy-start
  35.4 1.3 %collective-permute-start.5 = (f32[2,6,32,256]{3,2,1,0:T(8,128)}, f32[2,6,32,256]{3,2,1,0:T(8,128)S(1)}, u32[]{:S(2)}, u32[]{:S(2)}) collective-permute-start(f32[2,6,32,256]{3,2,1,0:T(8,128)} %refs_0_.1), channel_id=1, source_target_pairs={{24,0},{25,1},{26,2},{27,3},{28,4},{29,5},{30,6},{31,7}} | collective-permute-start | bytes 1179656 | tf_op jit(solution)/shard_map/ppermute | solution.py:25
  37.3 0.0 collective-permute-done.3.refs_5_
  37.3 0.0 collective-permute-done.2.refs_4_
  37.3 0.0 collective-permute-done.1.refs_3_
  37.4 5.8 %collective-permute-done.refs_2_ = f32[2,6,32,256]{3,2,1,0:T(8,128)S(1)} collective-permute-done((f32[2,6,32,256]{3,2,1,0:T(8,128)}, f32[2,6,32,256]{3,2,1,0:T(8,128)S(1)}, u32[]{:S(2)}, u32[]{:S(2)}) %collective-permute-start) | collective-permute-done | bytes 393248 | tf_op jit(solution)/shard_map/ppermute | solution.py:25
  43.1 4.9 %collective-permute-done.5.refs_7_ = f32[2,6,32,256]{3,2,1,0:T(8,128)S(1)} collective-permute-done((f32[2,6,32,256]{3,2,1,0:T(8,128)}, f32[2,6,32,256]{3,2,1,0:T(8,128)S(1)}, u32[]{:S(2)}, u32[]{:S(2)}) %collective-permute-start.5) | collective-permute-done | bytes 393248 | tf_op jit(solution)/shard_map/ppermute | solution.py:25
  48.2 0.7 copy-done.5
  48.8 22.3 %shard_map.50 = bf16[2,6,32,256]{3,2,1,0:T(8,128)(2,1)} custom-call(s32[1]{0:T(128)} %bitcast.first_ref, s32[1]{0:T(128)S(6)} %copy.28.deg_ref, f32[2,6,32,256]{3,2,1,0:T(8,128)} %refs_0_.1, f32[6,32,256]{2,1,0:T(8,128)} %refs_1_.1, f32[2,6,32,256]{3,2,1,0:T(8,128)} %copy-done.4, f32[2,6,32,256]{3,2,1,0:T(8,128)} %copy-done.3, f32[2,6,32,256]{3,2,1,0:T(8,128)} %copy-done.2, ...), custom_call_target="tpu_custom_call" | custom-call | tf_op jit(solution)/shard_map/pallas_call | solution.py:143
  71.1 1.0 %all_to_all.17 = bf16[2,8,6144]{2,1,0:T(8,128)(2,1)S(1)} reshape(bf16[2,6,32,256]{3,2,1,0:T(8,128)(2,1)} %shard_map.50) | data formatting | bytes 393216 | tf_op jit(solution)/shard_map/all_to_all | solution.py:181
  72.2 0.2 copy.19
  72.4 13.0 %all_to_all.24 = bf16[2,8,6144]{2,0,1:T(2,128)(2,1)S(1)} all-to-all(bf16[2,8,6144]{2,0,1:T(2,128)(2,1)S(1)} %copy.19), channel_id=1, replica_groups=mesh['dom'=4,'orb'=8] {'orb'}, dimensions={1} | all-to-all | bytes 393216 | tf_op jit(solution)/shard_map/all_to_all | solution.py:181
  85.4 0.1 copy.27
  85.4 0.2 copy.21
  85.6 0.1 reshape.24
  85.7 0.2 fusion
  86.0 9.0 %all_to_all.25 = f32[32,2,16]{2,1,0:T(2,128)S(1)} all-to-all(f32[32,2,16]{2,1,0:T(2,128)S(1)} %copy.22), channel_id=1, replica_groups=mesh['dom'=4,'orb'=8] {'orb','dom'}, dimensions={0} | all-to-all | bytes 8192 | tf_op jit(solution)/shard_map/all_to_all | solution.py:185
  95.0 0.6 broadcast_multiply_fusion
  (21 shorter events, 0.1 us)
Async XLA Ops:
  0.6 34.7 %collective-permute-start.4 = (f32[2,6,32,256]{3,2,1,0:T(8,128)}, f32[2,6,32,256]{3,2,1,0:T(8,128)S(1)}, u32[]{:S(2)}, u32[]{:S(2)}) collective-permute-start(f32[2,6,32,256]{3,2,1,0:T(8,128)} %refs_0_.1), channel_id=1, source_target_pairs={{16,0},{24,8},{17,1},{25,9},{18,2},{26,10},{19,3},{27,11},{20,4},{... | collective-permute-start | bytes 1179656 | tf_op jit(solution)/shard_map/ppermute | solution.py:25
  1.9 12.1 %collective-permute-start.8 = (f32[6,32,256]{2,1,0:T(8,128)}, f32[6,32,256]{2,1,0:T(8,128)S(1)}, u32[]{:S(2)}, u32[]{:S(2)}) collective-permute-start(f32[6,32,256]{2,1,0:T(8,128)} %refs_1_.1), channel_id=1, source_target_pairs={{8,0},{16,8},{24,16},{9,1},{17,9},{25,17},{10,2},{18,10},{26,18},{... | collective-permute-start | bytes 589832 | tf_op jit(solution)/shard_map/ppermute | solution.py:25
  3.2 15.3 %collective-permute-start.7 = (f32[6,32,256]{2,1,0:T(8,128)}, f32[6,32,256]{2,1,0:T(8,128)S(1)}, u32[]{:S(2)}, u32[]{:S(2)}) collective-permute-start(f32[6,32,256]{2,1,0:T(8,128)} %refs_1_.1), channel_id=1, source_target_pairs={{0,16},{8,24},{1,17},{9,25},{2,18},{10,26},{3,19},{11,27},{4,20},{... | collective-permute-start | bytes 589832 | tf_op jit(solution)/shard_map/ppermute | solution.py:25
  10.2 11.9 %collective-permute-start.6 = (f32[6,32,256]{2,1,0:T(8,128)}, f32[6,32,256]{2,1,0:T(8,128)S(1)}, u32[]{:S(2)}, u32[]{:S(2)}) collective-permute-start(f32[6,32,256]{2,1,0:T(8,128)} %refs_1_.1), channel_id=1, source_target_pairs={{0,8},{8,16},{16,24},{1,9},{9,17},{17,25},{2,10},{10,18},{18,26},{... | collective-permute-start | bytes 589832 | tf_op jit(solution)/shard_map/ppermute | solution.py:25
  12.7 10.9 %collective-permute-start.9 = (f32[6,32,256]{2,1,0:T(8,128)}, f32[6,32,256]{2,1,0:T(8,128)S(1)}, u32[]{:S(2)}, u32[]{:S(2)}) collective-permute-start(f32[6,32,256]{2,1,0:T(8,128)} %refs_1_.1), channel_id=1, source_target_pairs={{16,0},{24,8},{17,1},{25,9},{18,2},{26,10},{19,3},{27,11},{20,4},{... | collective-permute-start | bytes 589832 | tf_op jit(solution)/shard_map/ppermute | solution.py:25
  14.1 34.0 %copy-start.6 = (f32[6,32,256]{2,1,0:T(8,128)}, f32[6,32,256]{2,1,0:T(8,128)S(1)}, u32[]{:S(2)}) copy-start(f32[6,32,256]{2,1,0:T(8,128)S(1)} %collective-permute-done.8.refs_10_) | copy-start | bytes 589828
  14.1 23.2 %collective-permute-start.3 = (f32[2,6,32,256]{3,2,1,0:T(8,128)}, f32[2,6,32,256]{3,2,1,0:T(8,128)S(1)}, u32[]{:S(2)}, u32[]{:S(2)}) collective-permute-start(f32[2,6,32,256]{3,2,1,0:T(8,128)} %refs_0_.1), channel_id=1, source_target_pairs={{8,0},{16,8},{24,16},{9,1},{17,9},{25,17},{10,2},{18,10},{26,18},{... | collective-permute-start | bytes 1179656 | tf_op jit(solution)/shard_map/ppermute | solution.py:25
  18.6 29.5 %copy-start.7 = (f32[6,32,256]{2,1,0:T(8,128)}, f32[6,32,256]{2,1,0:T(8,128)S(1)}, u32[]{:S(2)}) copy-start(f32[6,32,256]{2,1,0:T(8,128)S(1)} %collective-permute-done.7.refs_9_) | copy-start | bytes 589828
  18.6 18.7 %collective-permute-start.2 = (f32[2,6,32,256]{3,2,1,0:T(8,128)}, f32[2,6,32,256]{3,2,1,0:T(8,128)S(1)}, u32[]{:S(2)}, u32[]{:S(2)}) collective-permute-start(f32[2,6,32,256]{3,2,1,0:T(8,128)} %refs_0_.1), channel_id=1, source_target_pairs={{0,24},{1,25},{2,26},{3,27},{4,28},{5,29},{6,30},{7,31}} | collective-permute-start | bytes 1179656 | tf_op jit(solution)/shard_map/ppermute | solution.py:25
  22.1 26.0 %copy-start.8 = (f32[6,32,256]{2,1,0:T(8,128)}, f32[6,32,256]{2,1,0:T(8,128)S(1)}, u32[]{:S(2)}) copy-start(f32[6,32,256]{2,1,0:T(8,128)S(1)} %collective-permute-done.6.refs_8_) | copy-start | bytes 589828
  22.1 15.3 %collective-permute-start.1 = (f32[2,6,32,256]{3,2,1,0:T(8,128)}, f32[2,6,32,256]{3,2,1,0:T(8,128)S(1)}, u32[]{:S(2)}, u32[]{:S(2)}) collective-permute-start(f32[2,6,32,256]{3,2,1,0:T(8,128)} %refs_0_.1), channel_id=1, source_target_pairs={{0,16},{8,24},{1,17},{9,25},{2,18},{10,26},{3,19},{11,27},{4,20},{... | collective-permute-start | bytes 1179656 | tf_op jit(solution)/shard_map/ppermute | solution.py:25
  23.6 24.5 %copy-start.9 = (f32[6,32,256]{2,1,0:T(8,128)}, f32[6,32,256]{2,1,0:T(8,128)S(1)}, u32[]{:S(2)}) copy-start(f32[6,32,256]{2,1,0:T(8,128)S(1)} %collective-permute-done.9.refs_11_) | copy-start | bytes 589828
  23.6 19.5 %collective-permute-start = (f32[2,6,32,256]{3,2,1,0:T(8,128)}, f32[2,6,32,256]{3,2,1,0:T(8,128)S(1)}, u32[]{:S(2)}, u32[]{:S(2)}) collective-permute-start(f32[2,6,32,256]{3,2,1,0:T(8,128)} %refs_0_.1), channel_id=1, source_target_pairs={{0,8},{8,16},{16,24},{1,9},{9,17},{17,25},{2,10},{10,18},{18,26},{... | collective-permute-start | bytes 1179656 | tf_op jit(solution)/shard_map/ppermute | solution.py:25
  35.3 12.8 %copy-start = (f32[2,6,32,256]{3,2,1,0:T(8,128)}, f32[2,6,32,256]{3,2,1,0:T(8,128)S(1)}, u32[]{:S(2)}) copy-start(f32[2,6,32,256]{3,2,1,0:T(8,128)S(1)} %collective-permute-done.4.refs_6_) | copy-start | bytes 1179652
  35.4 12.7 %collective-permute-start.5 = (f32[2,6,32,256]{3,2,1,0:T(8,128)}, f32[2,6,32,256]{3,2,1,0:T(8,128)S(1)}, u32[]{:S(2)}, u32[]{:S(2)}) collective-permute-start(f32[2,6,32,256]{3,2,1,0:T(8,128)} %refs_0_.1), channel_id=1, source_target_pairs={{24,0},{25,1},{26,2},{27,3},{28,4},{29,5},{30,6},{31,7}} | collective-permute-start | bytes 1179656 | tf_op jit(solution)/shard_map/ppermute | solution.py:25
  37.3 10.8 %copy-start.1 = (f32[2,6,32,256]{3,2,1,0:T(8,128)}, f32[2,6,32,256]{3,2,1,0:T(8,128)S(1)}, u32[]{:S(2)}) copy-start(f32[2,6,32,256]{3,2,1,0:T(8,128)S(1)} %collective-permute-done.3.refs_5_) | copy-start | bytes 1179652
  37.3 10.8 %copy-start.2 = (f32[2,6,32,256]{3,2,1,0:T(8,128)}, f32[2,6,32,256]{3,2,1,0:T(8,128)S(1)}, u32[]{:S(2)}) copy-start(f32[2,6,32,256]{3,2,1,0:T(8,128)S(1)} %collective-permute-done.2.refs_4_) | copy-start | bytes 1179652
  37.4 10.8 %copy-start.3 = (f32[2,6,32,256]{3,2,1,0:T(8,128)}, f32[2,6,32,256]{3,2,1,0:T(8,128)S(1)}, u32[]{:S(2)}) copy-start(f32[2,6,32,256]{3,2,1,0:T(8,128)S(1)} %collective-permute-done.1.refs_3_) | copy-start | bytes 1179652
  43.1 5.0 %copy-start.4 = (f32[2,6,32,256]{3,2,1,0:T(8,128)}, f32[2,6,32,256]{3,2,1,0:T(8,128)S(1)}, u32[]{:S(2)}) copy-start(f32[2,6,32,256]{3,2,1,0:T(8,128)S(1)} %collective-permute-done.refs_2_) | copy-start | bytes 1179652
  48.1 0.8 copy-start.5

commit v4 on v3

--- a/solution.py
+++ b/solution.py
@@ -1,5 +1,6 @@
 import functools
 
+import numpy as np
 import jax
 import jax.numpy as jnp
 from jax import lax
@@ -15,6 +16,14 @@
 SHIFT_C = 8.5
 HALF_W = 4.5
 RADIUS = len(STENCIL)
+
+
+def circulant(n):
+    gap = (np.arange(n)[None, :] - np.arange(n)[:, None]) % n
+    weights = np.zeros((n, n), np.float32)
+    for offset, weight in enumerate(STENCIL, 1):
+        weights[(gap == offset) | (gap == n - offset)] = np.float32(weight)
+    return weights
 
 
 def shifted(x, k):
@@ -39,12 +48,12 @@
     return below, above
 
 
-def filter_kernel(first_ref, deg_ref, *refs, n_orb_pieces, n_pot_pieces, grid_planes):
+def filter_kernel(first_ref, deg_ref, cz_ref, *refs, n_orb_pieces, n_pot_pieces, grid_planes):
     n_in = 2 + 2 * n_orb_pieces + 2 * n_pot_pieces
     ins = refs[:n_in]
     out_ref = refs[n_in]
-    cells_ref, pot_ref, sems = refs[n_in + 1], refs[n_in + 2], refs[n_in + 3]
-    iter_refs = refs[n_in + 4 :]
+    cells_ref, pot_ref, zsum_ref, sems = refs[n_in + 1 : n_in + 5]
+    iter_refs = refs[n_in + 5 :]
     orb_in, pot_in = ins[0], ins[1]
     orb_below = ins[2 : 2 + n_orb_pieces]
     orb_above = ins[2 + n_orb_pieces : 2 + 2 * n_orb_pieces]
@@ -95,18 +104,26 @@
         for offset, weight in enumerate(STENCIL, 1):
             beside_all = source[b, RADIUS + p + offset] + source[b, RADIUS + p - offset]
             beside_all = beside_all + pltpu.roll(field, offset, 0) + pltpu.roll(field, ny - offset, 0)
-            beside_all = beside_all + pltpu.roll(field, offset, 1) + pltpu.roll(field, nz - offset, 1)
             laplace = laplace + weight * beside_all
+        laplace = laplace + zsum_ref[b, p]
         applied = -0.5 * laplace + pot_ref[(order - 1) * RADIUS + p] * field
         if order == 1:
             return (applied - SHIFT_C * field) / HALF_W
         before = sources[order - 2][b, 2 * RADIUS + p]
         return 2.0 * (applied - SHIFT_C * field) / HALF_W - before
 
+    def along_z(order, planes):
+        source = sources[order - 1]
+        for b in range(block_orbs):
+            rows = source[b, RADIUS : RADIUS + planes].reshape(planes * ny, nz)
+            mixed = jnp.dot(rows, cz_ref[...], precision=lax.Precision.HIGHEST, preferred_element_type=jnp.float32)
+            zsum_ref[b, :planes] = mixed.reshape(planes, ny, nz)
+
     for order in range(1, DEG_MAX):
         margin = (DEG_MAX - order) * RADIUS
         dest = iter_refs[order - 1]
         planes = slab + 2 * margin
+        along_z(order, planes)
         for b in range(block_orbs):
             def body(p, carry, order=order, b=b, dest=dest):
                 value = plane_value(order, b, p)
@@ -115,8 +132,9 @@
                 keep = (keep >= 0) & (keep < grid_planes)
                 dest[b, p] = jnp.where(keep, value, 0.0)
                 return carry
-            lax.fori_loop(0, planes, body, 0)
-
+            lax.fori_loop(0, planes, body, 0, unroll=2)
+
+    along_z(DEG_MAX, slab)
     for b in range(block_orbs):
         def last(p, carry, b=b):
             value = plane_value(DEG_MAX, b, p)
@@ -127,7 +145,7 @@
             picked = jnp.where(levels >= DEG_MAX, value, picked)
             out_ref[b, p] = picked.astype(out_ref.dtype)
             return carry
-        lax.fori_loop(0, slab, last, 0)
+        lax.fori_loop(0, slab, last, 0, unroll=2)
 
 
 def chebyshev_filter(orbitals, potential, first, degree, grid_planes):
@@ -148,18 +166,19 @@
             grid_planes=grid_planes,
         ),
         out_shape=jax.ShapeDtypeStruct((block_orbs, slab, ny, nz), jnp.bfloat16),
-        in_specs=[smem, smem] + [hbm] * n_copies,
+        in_specs=[smem, smem, vmem] + [hbm] * n_copies,
         out_specs=vmem,
         scratch_shapes=[
             pltpu.VMEM((block_orbs, slab + 2 * reach, ny, nz), jnp.float32),
             pltpu.VMEM((slab + 2 * (reach - RADIUS), ny, nz), jnp.float32),
+            pltpu.VMEM((block_orbs, slab + 2 * (reach - RADIUS), ny, nz), jnp.float32),
             pltpu.SemaphoreType.DMA((n_copies,)),
         ]
         + [
             pltpu.VMEM((block_orbs, slab + 2 * (DEG_MAX - order) * RADIUS, ny, nz), jnp.float32)
             for order in range(1, DEG_MAX)
         ],
-    )(first, degree, *operands)
+    )(first, degree, jnp.asarray(circulant(nz)), *operands)
 
 
 def inner_rows(left, right):

time: 96 us -> 88.1 us (0.918)
  Pallas kernels: 22.3 us -> 14.4 us
    pallas_call x1, Pallas kernels: 22.3 us -> 14.4 us  [chebyshev_filter(): pl.pallas_call(functools.partial(filter_kernel, n_orb_pieces=len(orb_belo...]
where the time goes in v4:
time: 88.1 us; the launch traced here: 87.6 us
  starting transfers between devices  32.6 us (37%)
  blocking collectives  22 us (25%)
  Pallas kernels  14.4 us (16%)
  waiting for transfers between devices  13.9 us (16%)
  local copies, waits for them, and re-layouts  2.32 us (3%)
  between operations  1.57 us (2%)
    ppermute x10, starting transfers between devices, shifted(): return lax.ppermute(x, 'dom', pairs)  32.6 us
    pallas_call x1, Pallas kernels, chebyshev_filter(): pl.pallas_call(functools.partial(filter_kernel, n_orb_pieces=len(orb_belo...  14.4 us
    ppermute x10, waiting for transfers between devices, shifted(): return lax.ppermute(x, 'dom', pairs)  13.9 us
    all_to_all x1, blocking collectives, per_device(): lax.all_to_all(flattened, 'orb', split_axis=1, concat_axis=0, tiled=True)  13 us
    all_to_all x1, blocking collectives, per_device(): lax.all_to_all(sends, ('orb', 'dom'), split_axis=0, concat_axis=0, tiled=...  8.99 us
  transfers between devices with their start and end apart: 10, of which 3 were waited for; matrix products, arithmetic and copies ran while one was open for 0% of the time, Pallas kernels for 0%

profile of v4, /device:TPU:0, one launch (start us, length us, event | category | flops | bytes accessed | tf_op | source)
XLA Modules:
  0.0 87.6 jit_solution(9605382275643790613)
XLA Ops:
  0.6 1.3 %collective-permute-start.4 = (f32[2,6,32,256]{3,2,1,0:T(8,128)}, f32[2,6,32,256]{3,2,1,0:T(8,128)S(1)}, u32[]{:S(2)}, u32[]{:S(2)}) collective-permute-start(f32[2,6,32,256]{3,2,1,0:T(8,128)} %refs_0_.1), channel_id=1, source_target_pairs={{16,0},{24,8},{17,1},{25,9},{18,2},{26,10},{19,3},{27,11},{20,4},{... | collective-permute-start | bytes 1179656 | tf_op jit(solution)/shard_map/ppermute | solution.py:34
  1.9 1.3 %collective-permute-start.8 = (f32[6,32,256]{2,1,0:T(8,128)}, f32[6,32,256]{2,1,0:T(8,128)S(1)}, u32[]{:S(2)}, u32[]{:S(2)}) collective-permute-start(f32[6,32,256]{2,1,0:T(8,128)} %refs_1_.1), channel_id=1, source_target_pairs={{8,0},{16,8},{24,16},{9,1},{17,9},{25,17},{10,2},{18,10},{26,18},{... | collective-permute-start | bytes 589832 | tf_op jit(solution)/shard_map/ppermute | solution.py:34
  3.2 7.0 %collective-permute-start.7 = (f32[6,32,256]{2,1,0:T(8,128)}, f32[6,32,256]{2,1,0:T(8,128)S(1)}, u32[]{:S(2)}, u32[]{:S(2)}) collective-permute-start(f32[6,32,256]{2,1,0:T(8,128)} %refs_1_.1), channel_id=1, source_target_pairs={{0,16},{8,24},{1,17},{9,25},{2,18},{10,26},{3,19},{11,27},{4,20},{... | collective-permute-start | bytes 589832 | tf_op jit(solution)/shard_map/ppermute | solution.py:34
  10.2 2.5 %collective-permute-start.6 = (f32[6,32,256]{2,1,0:T(8,128)}, f32[6,32,256]{2,1,0:T(8,128)S(1)}, u32[]{:S(2)}, u32[]{:S(2)}) collective-permute-start(f32[6,32,256]{2,1,0:T(8,128)} %refs_1_.1), channel_id=1, source_target_pairs={{0,8},{8,16},{16,24},{1,9},{9,17},{17,25},{2,10},{10,18},{18,26},{... | collective-permute-start | bytes 589832 | tf_op jit(solution)/shard_map/ppermute | solution.py:34
  12.7 1.3 %collective-permute-start.9 = (f32[6,32,256]{2,1,0:T(8,128)}, f32[6,32,256]{2,1,0:T(8,128)S(1)}, u32[]{:S(2)}, u32[]{:S(2)}) collective-permute-start(f32[6,32,256]{2,1,0:T(8,128)} %refs_1_.1), channel_id=1, source_target_pairs={{16,0},{24,8},{17,1},{25,9},{18,2},{26,10},{19,3},{27,11},{20,4},{... | collective-permute-start | bytes 589832 | tf_op jit(solution)/shard_map/ppermute | solution.py:34
  14.0 0.0 collective-permute-done.8.refs_10_
  14.1 1.3 %collective-permute-start.3 = (f32[2,6,32,256]{3,2,1,0:T(8,128)}, f32[2,6,32,256]{3,2,1,0:T(8,128)S(1)}, u32[]{:S(2)}, u32[]{:S(2)}) collective-permute-start(f32[2,6,32,256]{3,2,1,0:T(8,128)} %refs_0_.1), channel_id=1, source_target_pairs={{8,0},{16,8},{24,16},{9,1},{17,9},{25,17},{10,2},{18,10},{26,18},{... | collective-permute-start | bytes 1179656 | tf_op jit(solution)/shard_map/ppermute | solution.py:34
  15.4 3.2 %collective-permute-done.7.refs_9_ = f32[6,32,256]{2,1,0:T(8,128)S(1)} collective-permute-done((f32[6,32,256]{2,1,0:T(8,128)}, f32[6,32,256]{2,1,0:T(8,128)S(1)}, u32[]{:S(2)}, u32[]{:S(2)}) %collective-permute-start.7) | collective-permute-done | bytes 196640 | tf_op jit(solution)/shard_map/ppermute | solution.py:34
  18.6 3.5 %collective-permute-start.2 = (f32[2,6,32,256]{3,2,1,0:T(8,128)}, f32[2,6,32,256]{3,2,1,0:T(8,128)S(1)}, u32[]{:S(2)}, u32[]{:S(2)}) collective-permute-start(f32[2,6,32,256]{3,2,1,0:T(8,128)} %refs_0_.1), channel_id=1, source_target_pairs={{0,24},{1,25},{2,26},{3,27},{4,28},{5,29},{6,30},{7,31}} | collective-permute-start | bytes 1179656 | tf_op jit(solution)/shard_map/ppermute | solution.py:34
  22.1 0.0 collective-permute-done.6.refs_8_
  22.1 1.5 %collective-permute-start.1 = (f32[2,6,32,256]{3,2,1,0:T(8,128)}, f32[2,6,32,256]{3,2,1,0:T(8,128)S(1)}, u32[]{:S(2)}, u32[]{:S(2)}) collective-permute-start(f32[2,6,32,256]{3,2,1,0:T(8,128)} %refs_0_.1), channel_id=1, source_target_pairs={{0,16},{8,24},{1,17},{9,25},{2,18},{10,26},{3,19},{11,27},{4,20},{... | collective-permute-start | bytes 1179656 | tf_op jit(solution)/shard_map/ppermute | solution.py:34
  23.6 0.0 collective-permute-done.9.refs_11_
  23.6 11.7 %collective-permute-start = (f32[2,6,32,256]{3,2,1,0:T(8,128)}, f32[2,6,32,256]{3,2,1,0:T(8,128)S(1)}, u32[]{:S(2)}, u32[]{:S(2)}) collective-permute-start(f32[2,6,32,256]{3,2,1,0:T(8,128)} %refs_0_.1), channel_id=1, source_target_pairs={{0,8},{8,16},{16,24},{1,9},{9,17},{17,25},{2,10},{10,18},{18,26},{... | collective-permute-start | bytes 1179656 | tf_op jit(solution)/shard_map/ppermute | solution.py:34
  35.3 0.0 collective-permute-done.4.refs_6_
  35.3 0.0 copy-start
  35.4 1.3 %collective-permute-start.5 = (f32[2,6,32,256]{3,2,1,0:T(8,128)}, f32[2,6,32,256]{3,2,1,0:T(8,128)S(1)}, u32[]{:S(2)}, u32[]{:S(2)}) collective-permute-start(f32[2,6,32,256]{3,2,1,0:T(8,128)} %refs_0_.1), channel_id=1, source_target_pairs={{24,0},{25,1},{26,2},{27,3},{28,4},{29,5},{30,6},{31,7}} | collective-permute-start | bytes 1179656 | tf_op jit(solution)/shard_map/ppermute | solution.py:34
  37.3 0.0 collective-permute-done.3.refs_5_
  37.3 0.0 collective-permute-done.2.refs_4_
  37.3 0.0 collective-permute-done.1.refs_3_
  37.4 5.8 %collective-permute-done.refs_2_ = f32[2,6,32,256]{3,2,1,0:T(8,128)S(1)} collective-permute-done((f32[2,6,32,256]{3,2,1,0:T(8,128)}, f32[2,6,32,256]{3,2,1,0:T(8,128)S(1)}, u32[]{:S(2)}, u32[]{:S(2)}) %collective-permute-start) | collective-permute-done | bytes 393248 | tf_op jit(solution)/shard_map/ppermute | solution.py:34
  43.1 4.9 %collective-permute-done.5.refs_7_ = f32[2,6,32,256]{3,2,1,0:T(8,128)S(1)} collective-permute-done((f32[2,6,32,256]{3,2,1,0:T(8,128)}, f32[2,6,32,256]{3,2,1,0:T(8,128)S(1)}, u32[]{:S(2)}, u32[]{:S(2)}) %collective-permute-start.5) | collective-permute-done | bytes 393248 | tf_op jit(solution)/shard_map/ppermute | solution.py:34
  48.2 0.7 copy-done.5
  48.8 14.4 %shard_map.59 = bf16[2,6,32,256]{3,2,1,0:T(8,128)(2,1)} custom-call(s32[1]{0:T(128)} %bitcast.first_ref, s32[1]{0:T(128)S(6)} %copy.29.deg_ref, f32[256,256]{1,0:T(8,128)} %constant.17.clone.cz_ref, f32[2,6,32,256]{3,2,1,0:T(8,128)} %refs_0_.1, f32[6,32,256]{2,1,0:T(8,128)} %refs_1_.1, f32[2,6,32,256]{3,2,1,0:T(8,128)} %copy-done.4, ...), custom_call_target="tpu_custom_call" | custom-call | tf_op jit(solution)/shard_map/pallas_call | solution.py:161
  63.2 1.0 %all_to_all.17 = bf16[2,8,6144]{2,1,0:T(8,128)(2,1)S(1)} reshape(bf16[2,6,32,256]{3,2,1,0:T(8,128)(2,1)} %shard_map.59) | data formatting | bytes 393216 | tf_op jit(solution)/shard_map/all_to_all | solution.py:200
  64.2 0.2 copy.20
  64.4 13.0 %all_to_all.24 = bf16[2,8,6144]{2,0,1:T(2,128)(2,1)S(1)} all-to-all(bf16[2,8,6144]{2,0,1:T(2,128)(2,1)S(1)} %copy.20), channel_id=1, replica_groups=mesh['dom'=4,'orb'=8] {'orb'}, dimensions={1} | all-to-all | bytes 393216 | tf_op jit(solution)/shard_map/all_to_all | solution.py:200
  77.4 0.1 copy.28
  77.5 0.2 copy.22
  77.7 0.1 reshape.24
  77.8 0.2 fusion
  78.0 9.0 %all_to_all.25 = f32[32,2,16]{2,1,0:T(2,128)S(1)} all-to-all(f32[32,2,16]{2,1,0:T(2,128)S(1)} %copy.23), channel_id=1, replica_groups=mesh['dom'=4,'orb'=8] {'orb','dom'}, dimensions={0} | all-to-all | bytes 8192 | tf_op jit(solution)/shard_map/all_to_all | solution.py:204
  87.1 0.6 broadcast_multiply_fusion
  (21 shorter events, 0.1 us)
Async XLA Ops:
  0.6 34.7 %collective-permute-start.4 = (f32[2,6,32,256]{3,2,1,0:T(8,128)}, f32[2,6,32,256]{3,2,1,0:T(8,128)S(1)}, u32[]{:S(2)}, u32[]{:S(2)}) collective-permute-start(f32[2,6,32,256]{3,2,1,0:T(8,128)} %refs_0_.1), channel_id=1, source_target_pairs={{16,0},{24,8},{17,1},{25,9},{18,2},{26,10},{19,3},{27,11},{20,4},{... | collective-permute-start | bytes 1179656 | tf_op jit(solution)/shard_map/ppermute | solution.py:34
  1.9 12.1 %collective-permute-start.8 = (f32[6,32,256]{2,1,0:T(8,128)}, f32[6,32,256]{2,1,0:T(8,128)S(1)}, u32[]{:S(2)}, u32[]{:S(2)}) collective-permute-start(f32[6,32,256]{2,1,0:T(8,128)} %refs_1_.1), channel_id=1, source_target_pairs={{8,0},{16,8},{24,16},{9,1},{17,9},{25,17},{10,2},{18,10},{26,18},{... | collective-permute-start | bytes 589832 | tf_op jit(solution)/shard_map/ppermute | solution.py:34
  3.2 15.3 %collective-permute-start.7 = (f32[6,32,256]{2,1,0:T(8,128)}, f32[6,32,256]{2,1,0:T(8,128)S(1)}, u32[]{:S(2)}, u32[]{:S(2)}) collective-permute-start(f32[6,32,256]{2,1,0:T(8,128)} %refs_1_.1), channel_id=1, source_target_pairs={{0,16},{8,24},{1,17},{9,25},{2,18},{10,26},{3,19},{11,27},{4,20},{... | collective-permute-start | bytes 589832 | tf_op jit(solution)/shard_map/ppermute | solution.py:34
  10.2 11.9 %collective-permute-start.6 = (f32[6,32,256]{2,1,0:T(8,128)}, f32[6,32,256]{2,1,0:T(8,128)S(1)}, u32[]{:S(2)}, u32[]{:S(2)}) collective-permute-start(f32[6,32,256]{2,1,0:T(8,128)} %refs_1_.1), channel_id=1, source_target_pairs={{0,8},{8,16},{16,24},{1,9},{9,17},{17,25},{2,10},{10,18},{18,26},{... | collective-permute-start | bytes 589832 | tf_op jit(solution)/shard_map/ppermute | solution.py:34
  12.7 10.9 %collective-permute-start.9 = (f32[6,32,256]{2,1,0:T(8,128)}, f32[6,32,256]{2,1,0:T(8,128)S(1)}, u32[]{:S(2)}, u32[]{:S(2)}) collective-permute-start(f32[6,32,256]{2,1,0:T(8,128)} %refs_1_.1), channel_id=1, source_target_pairs={{16,0},{24,8},{17,1},{25,9},{18,2},{26,10},{19,3},{27,11},{20,4},{... | collective-permute-start | bytes 589832 | tf_op jit(solution)/shard_map/ppermute | solution.py:34
  14.1 34.0 %copy-start.6 = (f32[6,32,256]{2,1,0:T(8,128)}, f32[6,32,256]{2,1,0:T(8,128)S(1)}, u32[]{:S(2)}) copy-start(f32[6,32,256]{2,1,0:T(8,128)S(1)} %collective-permute-done.8.refs_10_) | copy-start | bytes 589828
  14.1 23.2 %collective-permute-start.3 = (f32[2,6,32,256]{3,2,1,0:T(8,128)}, f32[2,6,32,256]{3,2,1,0:T(8,128)S(1)}, u32[]{:S(2)}, u32[]{:S(2)}) collective-permute-start(f32[2,6,32,256]{3,2,1,0:T(8,128)} %refs_0_.1), channel_id=1, source_target_pairs={{8,0},{16,8},{24,16},{9,1},{17,9},{25,17},{10,2},{18,10},{26,18},{... | collective-permute-start | bytes 1179656 | tf_op jit(solution)/shard_map/ppermute | solution.py:34
  18.6 29.5 %copy-start.7 = (f32[6,32,256]{2,1,0:T(8,128)}, f32[6,32,256]{2,1,0:T(8,128)S(1)}, u32[]{:S(2)}) copy-start(f32[6,32,256]{2,1,0:T(8,128)S(1)} %collective-permute-done.7.refs_9_) | copy-start | bytes 589828
  18.6 18.7 %collective-permute-start.2 = (f32[2,6,32,256]{3,2,1,0:T(8,128)}, f32[2,6,32,256]{3,2,1,0:T(8,128)S(1)}, u32[]{:S(2)}, u32[]{:S(2)}) collective-permute-start(f32[2,6,32,256]{3,2,1,0:T(8,128)} %refs_0_.1), channel_id=1, source_target_pairs={{0,24},{1,25},{2,26},{3,27},{4,28},{5,29},{6,30},{7,31}} | collective-permute-start | bytes 1179656 | tf_op jit(solution)/shard_map/ppermute | solution.py:34
  22.1 26.0 %copy-start.8 = (f32[6,32,256]{2,1,0:T(8,128)}, f32[6,32,256]{2,1,0:T(8,128)S(1)}, u32[]{:S(2)}) copy-start(f32[6,32,256]{2,1,0:T(8,128)S(1)} %collective-permute-done.6.refs_8_) | copy-start | bytes 589828
  22.1 15.3 %collective-permute-start.1 = (f32[2,6,32,256]{3,2,1,0:T(8,128)}, f32[2,6,32,256]{3,2,1,0:T(8,128)S(1)}, u32[]{:S(2)}, u32[]{:S(2)}) collective-permute-start(f32[2,6,32,256]{3,2,1,0:T(8,128)} %refs_0_.1), channel_id=1, source_target_pairs={{0,16},{8,24},{1,17},{9,25},{2,18},{10,26},{3,19},{11,27},{4,20},{... | collective-permute-start | bytes 1179656 | tf_op jit(solution)/shard_map/ppermute | solution.py:34
  23.6 24.5 %copy-start.9 = (f32[6,32,256]{2,1,0:T(8,128)}, f32[6,32,256]{2,1,0:T(8,128)S(1)}, u32[]{:S(2)}) copy-start(f32[6,32,256]{2,1,0:T(8,128)S(1)} %collective-permute-done.9.refs_11_) | copy-start | bytes 589828
  23.6 19.5 %collective-permute-start = (f32[2,6,32,256]{3,2,1,0:T(8,128)}, f32[2,6,32,256]{3,2,1,0:T(8,128)S(1)}, u32[]{:S(2)}, u32[]{:S(2)}) collective-permute-start(f32[2,6,32,256]{3,2,1,0:T(8,128)} %refs_0_.1), channel_id=1, source_target_pairs={{0,8},{8,16},{16,24},{1,9},{9,17},{17,25},{2,10},{10,18},{18,26},{... | collective-permute-start | bytes 1179656 | tf_op jit(solution)/shard_map/ppermute | solution.py:34
  35.3 12.8 %copy-start = (f32[2,6,32,256]{3,2,1,0:T(8,128)}, f32[2,6,32,256]{3,2,1,0:T(8,128)S(1)}, u32[]{:S(2)}) copy-start(f32[2,6,32,256]{3,2,1,0:T(8,128)S(1)} %collective-permute-done.4.refs_6_) | copy-start | bytes 1179652
  35.4 12.7 %collective-permute-start.5 = (f32[2,6,32,256]{3,2,1,0:T(8,128)}, f32[2,6,32,256]{3,2,1,0:T(8,128)S(1)}, u32[]{:S(2)}, u32[]{:S(2)}) collective-permute-start(f32[2,6,32,256]{3,2,1,0:T(8,128)} %refs_0_.1), channel_id=1, source_target_pairs={{24,0},{25,1},{26,2},{27,3},{28,4},{29,5},{30,6},{31,7}} | collective-permute-start | bytes 1179656 | tf_op jit(solution)/shard_map/ppermute | solution.py:34
  37.3 10.8 %copy-start.1 = (f32[2,6,32,256]{3,2,1,0:T(8,128)}, f32[2,6,32,256]{3,2,1,0:T(8,128)S(1)}, u32[]{:S(2)}) copy-start(f32[2,6,32,256]{3,2,1,0:T(8,128)S(1)} %collective-permute-done.3.refs_5_) | copy-start | bytes 1179652
  37.3 10.8 %copy-start.2 = (f32[2,6,32,256]{3,2,1,0:T(8,128)}, f32[2,6,32,256]{3,2,1,0:T(8,128)S(1)}, u32[]{:S(2)}) copy-start(f32[2,6,32,256]{3,2,1,0:T(8,128)S(1)} %collective-permute-done.2.refs_4_) | copy-start | bytes 1179652
  37.4 10.8 %copy-start.3 = (f32[2,6,32,256]{3,2,1,0:T(8,128)}, f32[2,6,32,256]{3,2,1,0:T(8,128)S(1)}, u32[]{:S(2)}) copy-start(f32[2,6,32,256]{3,2,1,0:T(8,128)S(1)} %collective-permute-done.1.refs_3_) | copy-start | bytes 1179652
  43.1 5.0 %copy-start.4 = (f32[2,6,32,256]{3,2,1,0:T(8,128)}, f32[2,6,32,256]{3,2,1,0:T(8,128)S(1)}, u32[]{:S(2)}) copy-start(f32[2,6,32,256]{3,2,1,0:T(8,128)S(1)} %collective-permute-done.refs_2_) | copy-start | bytes 1179652
  48.1 0.8 copy-start.5
